TPU v7x, 256 devices: a whole 4x4x8 slice. The times are simulated.
256 devices in a mesh: space: 64 (over y, z, core), pa: 2 (over x_lo), pb: 2 (over x_hi).
Axes of the slice: x: 4 (x_hi: 2, x_lo: 2; x = x_hi * 2 + x_lo), y: 4, z: 8, core: 2. Of those that a mesh axis runs over, the one named last changes fastest.
Arguments:
- field: float32 [8192, 16, 16, 16, 16], P('space', 'pa', None, 'pb'), may hold values from -6 to 6
- g_first: float32 [16, 128], P('pa'), may hold values from -1.5 to 1.5
- g_second: float32 [16, 128], replicated, may hold values from -1.5 to 1.5
- g_third: float32 [16, 128], P('pb'), may hold values from -1.5 to 1.5
- g_fourth: float32 [16, 128], replicated, may hold values from -1.5 to 1.5
- h_second: float32 [16, 128], replicated, may hold values from -1.5 to 1.5
- h_third: float32 [16, 128], P('pb'), may hold values from -1.5 to 1.5
- h_fourth: float32 [16, 128], replicated, may hold values from -1.5 to 1.5
Outputs:
- basis: float32 [8192, 128], P('space')
- core: float32 [128, 16, 16, 16, 16], P('space', 'pa', None, 'pb')
- next_sketch: float32 [128, 16, 128], P('space', 'pa')
All inputs are finite; a program needn't handle non-finite values.
Results may differ from a plain program's by a relative error of at most 0.00011.
Values sent between devices are 32-bit elements; how exact they have to be, the bound alone decides.
No kernel may reach another device: no remote copies, remote signals or barrier semaphores. Data moves between devices by JAX's collectives and lax.ppermute only.
A program may use at most 128 MiB of HBM per device.

v0:
```python
import jax
import jax.numpy as jnp
from jax import lax
from jax.sharding import PartitionSpec as P

MODE = 16
RANK = 128


def body(field, g_first, g_second, g_third, g_fourth, h_second, h_third, h_fourth):
    highest = lax.Precision.HIGHEST
    rows = field.shape[0]
    first_loc = field.shape[1]
    third_loc = field.shape[3]
    width = first_loc * MODE * third_loc * MODE
    flat = field.reshape(rows, width)
    omega = (
        g_first[:, None, None, None, :]
        * g_second[None, :, None, None, :]
        * g_third[None, None, :, None, :]
        * g_fourth[None, None, None, :, :]
    ).reshape(width, RANK)
    partial_sketch = jnp.dot(flat, omega, precision=highest, preferred_element_type=jnp.float32)
    sketch = lax.psum(partial_sketch, ("pa", "pb"))
    gram = lax.psum(
        jnp.dot(sketch.T, sketch, precision=highest, preferred_element_type=jnp.float32), "space"
    )
    lower = jnp.linalg.cholesky(gram)
    basis = lax.linalg.triangular_solve(
        lower, sketch, left_side=False, lower=True, transpose_a=True
    )
    core_flat = lax.psum_scatter(
        lax.dot_general(
            basis,
            flat,
            (((0,), (0,)), ((), ())),
            precision=highest,
            preferred_element_type=jnp.float32,
        ),
        "space",
        scatter_dimension=0,
        tiled=True,
    )
    own_rank = core_flat.shape[0]
    psi = (
        h_second[:, None, None, :] * h_third[None, :, None, :] * h_fourth[None, None, :, :]
    ).reshape(MODE * third_loc * MODE, RANK)
    partial_next = jnp.dot(
        core_flat.reshape(own_rank * first_loc, MODE * third_loc * MODE),
        psi,
        precision=highest,
        preferred_element_type=jnp.float32,
    )
    next_sketch = lax.psum(partial_next, "pb")
    core = core_flat.reshape(own_rank, first_loc, MODE, third_loc, MODE)
    return (basis, core, next_sketch.reshape(own_rank, first_loc, RANK))


def solution(mesh):
    placed = (
        P("space", "pa", None, "pb", None),
        P("pa", None),
        P(),
        P("pb", None),
        P(),
        P(),
        P("pb", None),
        P(),
    )
    return jax.shard_map(
        body,
        mesh=mesh,
        in_specs=placed,
        out_specs=(P("space", None), P("space", "pa", None, "pb", None), P("space", "pa", None)),
        check_vma=False,
    )
```

profile of v0, /device:TPU:24, one launch (start us, length us, event | category | flops | bytes accessed | tf_op | source)
XLA Modules:
  0.0 505.9 jit_solution(7857300615730254369)
XLA Ops:
  7.2 0.7 broadcast_multiply_fusion.3
  7.9 0.7 broadcast_multiply_fusion.1
  8.6 16.7 %fusion.4 = f32[128,128]{0,1:T(8,128)} fusion(f32[128,8,16,8,16]{0,4,3,2,1:T(8,128)} %param.8, f32[16,128]{1,0:T(8,128)} %param.12, f32[8,16,8,128]{3,2,1,0:T(8,128)S(1)} %broadcast_multiply_fusion.1), kind=kOutput, calls=%fused_computation.4 | convolution fusion | flops 3223322624 | bytes 8986624 | tf_op jit(solution)/shard_map/dot_general | solution.py:23
  25.4 49.0 %all-reduce.5.cloned.1.call-done = f32[128,128]{0,1:T(8,128)} async-done(((f32[128,128]{0,1:T(8,128)}), f32[128,128]{0,1:T(8,128)}) %all-reduce.5.cloned.1.call-update) | async-done | bytes 65552 | tf_op jit(solution)/shard_map/psum | solution.py:24
  74.5 1.8 fusion.11
  76.3 0.2 all-reduce.9.cloned.1.call-start
  76.5 172.9 %all-reduce.7.cloned.1.call-done = f32[128,128]{0,1:T(8,128)} async-done(((f32[128,128]{0,1:T(8,128)}), f32[128,128]{0,1:T(8,128)}) %all-reduce.7.cloned.1.call-update) | async-done | bytes 65552 | tf_op jit(solution)/shard_map/psum | solution.py:25
  249.4 0.9 copy.14
  250.4 0.9 fusion.10
  251.2 11.7 %cholesky.16 = f32[128,128]{1,0:T(8,128)S(1)} custom-call(f32[128,128]{1,0:T(8,128)S(1)} %fusion.10), custom_call_target="Cholesky" | custom-call | tf_op jit(solution)/shard_map/jit(cholesky)/cholesky | solution.py:28
  263.0 0.6 compare_reduce_fusion
  263.6 0.7 fusion.7
  264.3 9.8 %custom-call.6 = f32[1,128,128]{1,2,0:T(8,128)S(1)} custom-call(f32[1,128,128]{2,1,0:T(8,128)S(1)} %fusion.7), custom_call_target="InvertDiagBlocksLowerTriangular" | custom-call | tf_op jit(solution)/shard_map/triangular_solve | solution.py:29
  274.1 1.1 fusion.8
  275.2 12.1 %fusion.12 = f32[128,16384]{1,0:T(8,128)} fusion(f32[128,128]{1,0:T(8,128)S(1)} %fusion.8, f32[128,16384]{0,1:T(8,128)} %bitcast.28), kind=kOutput, calls=%fused_computation.22 | convolution fusion | flops 3221225472 | bytes 16842752 | tf_op jit(solution)/shard_map/dot_general | solution.py:33
  287.3 0.6 copy-done.4
  288.0 0.6 dynamic-slice
  289.2 0.1 broadcast_multiply_fusion
  289.4 199.7 %all-reduce.9.cloned.1.call-done = f32[128,16384]{1,0:T(8,128)} async-done(((f32[128,16384]{1,0:T(8,128)}), f32[128,16384]{1,0:T(8,128)}) %all-reduce.9.cloned.1.call-update) | async-done | bytes 8388624
  489.0 1.1 constant_dynamic-slice_fusion
  490.1 0.1 reshape.68
  490.3 1.4 reshape.67
  491.6 0.6 convolution_bitcast_fusion
  492.2 7.1 %psum.23 = f32[2,8,128]{2,1,0:T(8,128)} all-reduce(f32[2,8,128]{2,1,0:T(8,128)S(1)} %convolution_bitcast_fusion), channel_id=1, replica_groups=mesh['space'=64,'pa'=2,'pb'=2] {'pb'}, use_global_device_ids=true, to_apply=%region_5.6 | all-reduce | flops 2048 | bytes 16384 | tf_op jit(solution)/shard_map/psum | solution.py:54
  (16 shorter events, 0.2 us)
Async XLA Ops:
  7.2 67.3 %all-reduce.5.cloned.1.call-start = ((), (), s32[]{:S(2)}) async-start(), calls=%async_computation | async-start | bytes 131072 | tf_op jit(solution)/shard_map/psum | solution.py:24
  25.4 224.0 %all-reduce.7.cloned.1.call-start = ((), (), s32[]{:S(2)}) async-start(), calls=%async_computation.1 | async-start | bytes 131072 | tf_op jit(solution)/shard_map/psum | solution.py:25
  76.3 412.7 %all-reduce.9.cloned.1.call-start = ((), (), s32[]{:S(2)}) async-start(), calls=%async_computation.2 | async-start | bytes 16777216
  275.2 12.1 %copy-start = (f32[128,128]{1,0:T(8,128)}, f32[128,128]{1,0:T(8,128)S(1)}, u32[]{:S(2)}) copy-start(f32[128,128]{1,0:T(8,128)S(1)} %fusion.8) | copy-start | bytes 196612
  287.3 0.7 copy-start.4
  287.3 1.9 copy-start.2
  287.3 1.9 copy-start.3
  287.3 1.9 copy-start.1
Sparse Core Ops, SparseCore 0:
  25.5 48.9 all-reduce.4
  78.5 170.8 all-reduce.6
  287.5 201.5 all-reduce.8
where the time goes:
time: 508 us; the launch traced here: 506 us
  waiting for transfers between devices  422 us (83%)
  matrix products  32.3 us (6%)
  other arithmetic  25.3 us (5%)
  between operations  14.5 us (3%)
  blocking collectives  7.1 us (1%)
    unnamed x4, waiting for transfers between devices  200 us
    psum x1, waiting for transfers between devices, body(): lax.psum(jnp.dot(sketch.T, sketch, precision=highest, preferred_element_t...  173 us
    psum x1, waiting for transfers between devices, body(): sketch = lax.psum(partial_sketch, ('pa', 'pb'))  49 us
    dot_general x1, matrix products, body(): jnp.dot(flat, omega, precision=highest, preferred_element_type=jnp.float32)  16.7 us
    another operation x3, other arithmetic, body(): lower = jnp.linalg.cholesky(gram)  12.4 us
    dot_general x1, matrix products, body(): lax.dot_general(basis, flat, (((0,), (0,)), ((), ())), precision=highest,...  12.1 us
    another operation x2, other arithmetic, body(): lax.linalg.triangular_solve(lower, sketch, left_side=False, lower=True, t...  10.5 us
  transfers between devices with their start and end apart: 3, of which 3 were waited for; matrix products, arithmetic and copies ran while one was open for 0% of the time, Pallas kernels for 0%

commit v1 on v0

--- a/solution.py
+++ b/solution.py
@@ -1,4 +1,5 @@
 import jax
+import numpy as np
 import jax.numpy as jnp
 from jax import lax
 from jax.sharding import PartitionSpec as P
@@ -7,7 +8,36 @@
 RANK = 128
 
 
-def body(field, g_first, g_second, g_third, g_fourth, h_second, h_third, h_fourth):
+def butterfly_sum(x, axis, size):
+    step = 1
+    while step < size:
+        x = x + lax.ppermute(x, axis, [(i, i ^ step) for i in range(size)])
+        step *= 2
+    return x
+
+
+def bit_reverse(value, bits):
+    out = 0
+    for _ in range(bits):
+        out = (out << 1) | (value & 1)
+        value >>= 1
+    return out
+
+
+def halving_scatter(x, axis, size):
+    idx = lax.axis_index(axis)
+    step = 1
+    while step < size:
+        half = x.shape[0] // 2
+        bit = (idx // step) % 2
+        keep = lax.dynamic_slice_in_dim(x, bit * half, half, 0)
+        send = lax.dynamic_slice_in_dim(x, (1 - bit) * half, half, 0)
+        x = keep + lax.ppermute(send, axis, [(i, i ^ step) for i in range(size)])
+        step *= 2
+    return x
+
+
+def body(field, g_first, g_second, g_third, g_fourth, h_second, h_third, h_fourth, *, n_space, n_pa, n_pb):
     highest = lax.Precision.HIGHEST
     rows = field.shape[0]
     first_loc = field.shape[1]
@@ -21,25 +51,27 @@
         * g_fourth[None, None, None, :, :]
     ).reshape(width, RANK)
     partial_sketch = jnp.dot(flat, omega, precision=highest, preferred_element_type=jnp.float32)
-    sketch = lax.psum(partial_sketch, ("pa", "pb"))
-    gram = lax.psum(
-        jnp.dot(sketch.T, sketch, precision=highest, preferred_element_type=jnp.float32), "space"
+    sketch = butterfly_sum(butterfly_sum(partial_sketch, "pa", n_pa), "pb", n_pb)
+    gram = butterfly_sum(
+        jnp.dot(sketch.T, sketch, precision=highest, preferred_element_type=jnp.float32), "space", n_space
     )
     lower = jnp.linalg.cholesky(gram)
     basis = lax.linalg.triangular_solve(
         lower, sketch, left_side=False, lower=True, transpose_a=True
     )
-    core_flat = lax.psum_scatter(
+    bits = n_space.bit_length() - 1
+    per = RANK // n_space
+    order = np.array([per * bit_reverse(b, bits) + t for b in range(n_space) for t in range(per)])
+    core_flat = halving_scatter(
         lax.dot_general(
-            basis,
+            basis[:, order],
             flat,
             (((0,), (0,)), ((), ())),
             precision=highest,
             preferred_element_type=jnp.float32,
         ),
         "space",
-        scatter_dimension=0,
-        tiled=True,
+        n_space,
     )
     own_rank = core_flat.shape[0]
     psi = (
@@ -51,7 +83,7 @@
         precision=highest,
         preferred_element_type=jnp.float32,
     )
-    next_sketch = lax.psum(partial_next, "pb")
+    next_sketch = butterfly_sum(partial_next, "pb", n_pb)
     core = core_flat.reshape(own_rank, first_loc, MODE, third_loc, MODE)
     return (basis, core, next_sketch.reshape(own_rank, first_loc, RANK))
 
@@ -67,8 +99,9 @@
         P("pb", None),
         P(),
     )
+    sizes = dict(n_space=mesh.shape["space"], n_pa=mesh.shape["pa"], n_pb=mesh.shape["pb"])
     return jax.shard_map(
-        body,
+        lambda *a: body(*a, **sizes),
         mesh=mesh,
         in_specs=placed,
         out_specs=(P("space", None), P("space", "pa", None, "pb", None), P("space", "pa", None)),

time: 508 us -> 264 us (0.52)
  waiting for transfers between devices: 422 us -> 157 us
  starting transfers between devices: 0.3 us -> 34.9 us
  between operations: 14.5 us -> 0.9 us
  other arithmetic: 25.3 us -> 33 us
  blocking collectives: 7.1 us -> 0 us
    psum x2 -> x0, waiting for transfers between devices: 222 us -> none  [the longest x1 173 us: body(): lax.psum(jnp.dot(sketch.T, sketch, precision=highest, preferred_element_t...]
    unnamed x4 -> x0, waiting for transfers between devices: 200 us -> none
    ppermute x0 -> x15, waiting for transfers between devices: none -> 157 us  [the longest x6 135 us: halving_scatter(): x = keep + lax.ppermute(send, axis, [(i, i ^ step) for i in range(size)])]
    ppermute x0 -> x15, starting transfers between devices: none -> 34.9 us  [the longest x9 22.9 us: butterfly_sum(): x = x + lax.ppermute(x, axis, [(i, i ^ step) for i in range(size)])]
    add x0 -> x14, other arithmetic: none -> 7.93 us  [the longest x6 7.86 us: halving_scatter(): x = keep + lax.ppermute(send, axis, [(i, i ^ step) for i in range(size)])]
    psum x1 -> x0, blocking collectives: 7.1 us -> none  [body(): next_sketch = lax.psum(partial_next, 'pb')]
  transfers between devices with their start and end apart: 3 -> 15, of which waited for: 3 -> 15; matrix products, arithmetic and copies ran while one was open for 0% -> 1% of each run, Pallas kernels for 0% -> 0%
where the time goes in v1:
time: 264 us; the launch traced here: 263 us
  waiting for transfers between devices  157 us (59%)
  starting transfers between devices  34.9 us (13%)
  other arithmetic  33 us (12%)
  matrix products  27.6 us (10%)
  local copies, waits for them, and re-layouts  9.15 us (3%)
    ppermute x6, waiting for transfers between devices, halving_scatter(): x = keep + lax.ppermute(send, axis, [(i, i ^ step) for i in range(size)])  135 us
    ppermute x9, starting transfers between devices, butterfly_sum(): x = x + lax.ppermute(x, axis, [(i, i ^ step) for i in range(size)])  22.9 us
    ppermute x9, waiting for transfers between devices, butterfly_sum(): x = x + lax.ppermute(x, axis, [(i, i ^ step) for i in range(size)])  22.8 us
    dot_general x1, matrix products, body(): jnp.dot(flat, omega, precision=highest, preferred_element_type=jnp.float32)  16.1 us
    another operation x3, other arithmetic, body(): lower = jnp.linalg.cholesky(gram)  12.4 us
    ppermute x6, starting transfers between devices, halving_scatter(): x = keep + lax.ppermute(send, axis, [(i, i ^ step) for i in range(size)])  11.9 us
    another operation x2, other arithmetic, body(): lax.linalg.triangular_solve(lower, sketch, left_side=False, lower=True, t...  10.5 us
    dot_general x1, matrix products, body(): lax.dot_general(basis[:, order], flat, (((0,), (0,)), ((), ())), precisio...  10.3 us
  transfers between devices with their start and end apart: 15, of which 15 were waited for; matrix products, arithmetic and copies ran while one was open for 1% of the time, Pallas kernels for 0%

profile of v1, /device:TPU:24, one launch (start us, length us, event | category | flops | bytes accessed | tf_op | source)
XLA Modules:
  0.0 262.9 jit_solution(15171853526205542024)
XLA Ops:
  2.1 16.1 %fusion.4 = f32[128,128]{0,1:T(8,128)S(1)} fusion(f32[128,8,16,8,16]{0,4,3,2,1:T(8,128)} %param.10, f32[16,128]{1,0:T(8,128)} %param.14, f32[8,16,8,128]{3,2,1,0:T(8,128)S(1)} %broadcast_multiply_fusion.1), kind=kOutput, calls=%fused_computation.7 | convolution fusion | flops 3223322624 | bytes 8986624 | tf_op jit(solution)/shard_map/dot_general | solution.py:53
  19.8 2.8 %collective-permute-done = f32[128,128]{0,1:T(8,128)S(1)} collective-permute-done((f32[128,128]{0,1:T(8,128)S(1)}, f32[128,128]{0,1:T(8,128)S(1)}, u32[]{:S(2)}, u32[]{:S(2)}) %collective-permute-start) | collective-permute-done | bytes 65568 | tf_op jit(solution)/shard_map/ppermute | solution.py:14
  22.6 3.1 %collective-permute-start.1 = (f32[128,128]{0,1:T(8,128)S(1)}, f32[128,128]{0,1:T(8,128)S(1)}, u32[]{:S(2)}, u32[]{:S(2)}) collective-permute-start(f32[128,128]{0,1:T(8,128)S(1)} %add.123), channel_id=1, source_target_pairs={{0,1},{1,0},{2,3},{3,2},{4,5},{5,4},{6,7},{7,6},{8,9},{9,8},{10,11... | collective-permute-start | bytes 196616 | tf_op jit(solution)/shard_map/ppermute | solution.py:14
  25.7 2.7 %collective-permute-done.1 = f32[128,128]{0,1:T(8,128)S(1)} collective-permute-done((f32[128,128]{0,1:T(8,128)S(1)}, f32[128,128]{0,1:T(8,128)S(1)}, u32[]{:S(2)}, u32[]{:S(2)}) %collective-permute-start.1) | collective-permute-done | bytes 65568 | tf_op jit(solution)/shard_map/ppermute | solution.py:14
  32.1 2.4 collective-permute-done.3
  34.5 3.4 %collective-permute-start.4 = (f32[128,128]{0,1:T(8,128)S(1)}, f32[128,128]{0,1:T(8,128)S(1)}, u32[]{:S(2)}, u32[]{:S(2)}) collective-permute-start(f32[128,128]{0,1:T(8,128)S(1)} %add.126), channel_id=1, source_target_pairs={{0,16},{4,20},{8,24},{12,28},{16,0},{20,4},{24,8},{28,12},{32,48},... | collective-permute-start | bytes 196616 | tf_op jit(solution)/shard_map/ppermute | solution.py:14
  37.9 2.6 collective-permute-done.4
  40.4 7.4 %collective-permute-start.5 = (f32[128,128]{0,1:T(8,128)S(1)}, f32[128,128]{0,1:T(8,128)S(1)}, u32[]{:S(2)}, u32[]{:S(2)}) collective-permute-start(f32[128,128]{0,1:T(8,128)S(1)} %add.127), channel_id=1, source_target_pairs={{0,32},{4,36},{8,40},{12,44},{16,48},{20,52},{24,56},{28,60},{32,0... | collective-permute-start | bytes 196616 | tf_op jit(solution)/shard_map/ppermute | solution.py:14
  50.9 3.5 %collective-permute-done.6 = f32[128,128]{0,1:T(8,128)S(1)} collective-permute-done((f32[128,128]{0,1:T(8,128)S(1)}, f32[128,128]{0,1:T(8,128)S(1)}, u32[]{:S(2)}, u32[]{:S(2)}) %collective-permute-start.6) | collective-permute-done | bytes 65568 | tf_op jit(solution)/shard_map/ppermute | solution.py:14
  55.9 4.5 %collective-permute-done.7 = f32[128,128]{0,1:T(8,128)S(1)} collective-permute-done((f32[128,128]{0,1:T(8,128)S(1)}, f32[128,128]{0,1:T(8,128)S(1)}, u32[]{:S(2)}, u32[]{:S(2)}) %collective-permute-start.7) | collective-permute-done | bytes 65568 | tf_op jit(solution)/shard_map/ppermute | solution.py:14
  60.6 11.7 %cholesky.16 = f32[128,128]{1,0:T(8,128)S(1)} custom-call(f32[128,128]{1,0:T(8,128)S(1)} %fusion.10), custom_call_target="Cholesky" | custom-call | tf_op jit(solution)/shard_map/jit(cholesky)/cholesky | solution.py:58
  73.6 9.8 %custom-call.6 = f32[1,128,128]{1,2,0:T(8,128)S(1)} custom-call(f32[1,128,128]{2,1,0:T(8,128)S(1)} %fusion.7), custom_call_target="InvertDiagBlocksLowerTriangular" | custom-call | tf_op jit(solution)/shard_map/triangular_solve | solution.py:59
  84.5 10.3 %fusion.12 = f32[128,16384]{1,0:T(8,128)S(1)} fusion(f32[128,128]{1,0:T(8,128)S(1)} %gather_fusion, f32[128,16384]{0,1:T(8,128)} %bitcast.27), kind=kOutput, calls=%fused_computation.35 | convolution fusion | flops 3221225472 | bytes 16842752 | tf_op jit(solution)/shard_map/dot_general | solution.py:66
  94.8 2.5 constant_dynamic-slice_fusion.5
  99.3 7.5 %collective-permute-done.8 = f32[64,16384]{1,0:T(8,128)} collective-permute-done((f32[64,16384]{1,0:T(8,128)}, f32[64,16384]{1,0:T(8,128)}, u32[]{:S(2)}, u32[]{:S(2)}) %collective-permute-start.8) | collective-permute-done | bytes 4194336 | tf_op jit(solution)/shard_map/ppermute | solution.py:35
  106.8 3.9 %dynamic-slice_add_fusion = f32[64,16384]{1,0:T(8,128)S(1)} fusion(f32[64,16384]{1,0:T(8,128)} %collective-permute-done.8, f32[128,16384]{1,0:T(8,128)} %copy-done, s32[]{:T(128)S(6)} %select_n.90), kind=kLoop, calls=%fused_computation.3 | loop fusion | flops 1048576 | bytes 12582916 | tf_op jit(solution)/shard_map/add | solution.py:35
  113.9 46.9 %collective-permute-done.9 = f32[32,16384]{1,0:T(8,128)} collective-permute-done((f32[32,16384]{1,0:T(8,128)S(1)}, f32[32,16384]{1,0:T(8,128)}, u32[]{:S(2)}, u32[]{:S(2)}) %collective-permute-start.9) | collective-permute-done | bytes 2097184 | tf_op jit(solution)/shard_map/ppermute | solution.py:35
  160.9 2.4 dynamic-slice_add_fusion.1
  165.6 45.7 %collective-permute-done.10 = f32[16,16384]{1,0:T(8,128)} collective-permute-done((f32[16,16384]{1,0:T(8,128)S(1)}, f32[16,16384]{1,0:T(8,128)}, u32[]{:S(2)}, u32[]{:S(2)}) %collective-permute-start.10) | collective-permute-done | bytes 1048608 | tf_op jit(solution)/shard_map/ppermute | solution.py:35
  212.7 5.8 %collective-permute-start.11 = (f32[8,16384]{1,0:T(8,128)S(1)}, f32[8,16384]{1,0:T(8,128)S(1)}, u32[]{:S(2)}, u32[]{:S(2)}) collective-permute-start(f32[8,16384]{1,0:T(8,128)S(1)} %constant_dynamic-slice_fusion.2), channel_id=1, source_target_pairs={{0,32},{4,36},{8,40},{12,44},{16,48},{20,52},{24,56},{28,60},{32,0... | collective-permute-start | bytes 1572872 | tf_op jit(solution)/shard_map/ppermute | solution.py:35
  218.5 23.5 %collective-permute-done.11 = f32[8,16384]{1,0:T(8,128)S(1)} collective-permute-done((f32[8,16384]{1,0:T(8,128)S(1)}, f32[8,16384]{1,0:T(8,128)S(1)}, u32[]{:S(2)}, u32[]{:S(2)}) %collective-permute-start.11) | collective-permute-done | bytes 524320 | tf_op jit(solution)/shard_map/ppermute | solution.py:35
  243.5 6.1 %collective-permute-done.12 = f32[4,16384]{1,0:T(4,128)S(1)} collective-permute-done((f32[4,16384]{1,0:T(4,128)S(1)}, f32[4,16384]{1,0:T(4,128)S(1)}, u32[]{:S(2)}, u32[]{:S(2)}) %collective-permute-start.12) | collective-permute-done | bytes 262176 | tf_op jit(solution)/shard_map/ppermute | solution.py:35
  251.3 4.9 %collective-permute-done.13 = f32[2,16384]{1,0:T(2,128)S(1)} collective-permute-done((f32[2,16384]{1,0:T(2,128)S(1)}, f32[2,16384]{1,0:T(2,128)S(1)}, u32[]{:S(2)}, u32[]{:S(2)}) %collective-permute-start.13) | collective-permute-done | bytes 131104 | tf_op jit(solution)/shard_map/ppermute | solution.py:35
  257.1 3.1 %collective-permute-start.14 = (f32[16,128]{1,0:T(8,128)S(1)}, f32[16,128]{1,0:T(8,128)S(1)}, u32[]{:S(2)}, u32[]{:S(2)}) collective-permute-start(f32[16,128]{1,0:T(8,128)S(1)} %fusion.13), channel_id=1, source_target_pairs={{0,1},{1,0},{2,3},{3,2},{4,5},{5,4},{6,7},{7,6},{8,9},{9,8},{10,11... | collective-permute-start | bytes 24584 | tf_op jit(solution)/shard_map/ppermute | solution.py:14
  (62 shorter events, 29.4 us)
Async XLA Ops:
  2.1 53.9 %copy-start.6 = (s32[128]{0:T(128)S(1)}, s32[128]{0:T(128)}, u32[]{:S(2)}) copy-start(s32[128]{0:T(128)} %constant.158) | copy-start | bytes 1540
  18.2 4.4 %collective-permute-start = (f32[128,128]{0,1:T(8,128)S(1)}, f32[128,128]{0,1:T(8,128)S(1)}, u32[]{:S(2)}, u32[]{:S(2)}) collective-permute-start(f32[128,128]{0,1:T(8,128)S(1)} %fusion.4), channel_id=1, source_target_pairs={{0,2},{2,0},{1,3},{3,1},{4,6},{6,4},{5,7},{7,5},{8,10},{10,8},{9,1... | collective-permute-start | bytes 196616 | tf_op jit(solution)/shard_map/ppermute | solution.py:14
  22.6 5.9 %collective-permute-start.1 = (f32[128,128]{0,1:T(8,128)S(1)}, f32[128,128]{0,1:T(8,128)S(1)}, u32[]{:S(2)}, u32[]{:S(2)}) collective-permute-start(f32[128,128]{0,1:T(8,128)S(1)} %add.123), channel_id=1, source_target_pairs={{0,1},{1,0},{2,3},{3,2},{4,5},{5,4},{6,7},{7,6},{8,9},{9,8},{10,11... | collective-permute-start | bytes 196616 | tf_op jit(solution)/shard_map/ppermute | solution.py:14
  28.7 1.3 collective-permute-start.2
  30.1 4.4 %collective-permute-start.3 = (f32[128,128]{0,1:T(8,128)S(1)}, f32[128,128]{0,1:T(8,128)S(1)}, u32[]{:S(2)}, u32[]{:S(2)}) collective-permute-start(f32[128,128]{0,1:T(8,128)S(1)} %add.125), channel_id=1, source_target_pairs={{0,8},{4,12},{8,0},{12,4},{16,24},{20,28},{24,16},{28,20},{32,40},... | collective-permute-start | bytes 196616 | tf_op jit(solution)/shard_map/ppermute | solution.py:14
  34.5 5.9 %collective-permute-start.4 = (f32[128,128]{0,1:T(8,128)S(1)}, f32[128,128]{0,1:T(8,128)S(1)}, u32[]{:S(2)}, u32[]{:S(2)}) collective-permute-start(f32[128,128]{0,1:T(8,128)S(1)} %add.126), channel_id=1, source_target_pairs={{0,16},{4,20},{8,24},{12,28},{16,0},{20,4},{24,8},{28,12},{32,48},... | collective-permute-start | bytes 196616 | tf_op jit(solution)/shard_map/ppermute | solution.py:14
  40.4 9.6 %collective-permute-start.5 = (f32[128,128]{0,1:T(8,128)S(1)}, f32[128,128]{0,1:T(8,128)S(1)}, u32[]{:S(2)}, u32[]{:S(2)}) collective-permute-start(f32[128,128]{0,1:T(8,128)S(1)} %add.127), channel_id=1, source_target_pairs={{0,32},{4,36},{8,40},{12,44},{16,48},{20,52},{24,56},{28,60},{32,0... | collective-permute-start | bytes 196616 | tf_op jit(solution)/shard_map/ppermute | solution.py:14
  50.1 4.4 %collective-permute-start.6 = (f32[128,128]{0,1:T(8,128)S(1)}, f32[128,128]{0,1:T(8,128)S(1)}, u32[]{:S(2)}, u32[]{:S(2)}) collective-permute-start(f32[128,128]{0,1:T(8,128)S(1)} %add.128), channel_id=1, source_target_pairs={{0,64},{4,68},{8,72},{12,76},{16,80},{20,84},{24,88},{28,92},{32,9... | collective-permute-start | bytes 196616 | tf_op jit(solution)/shard_map/ppermute | solution.py:14
  54.4 6.0 %collective-permute-start.7 = (f32[128,128]{0,1:T(8,128)S(1)}, f32[128,128]{0,1:T(8,128)S(1)}, u32[]{:S(2)}, u32[]{:S(2)}) collective-permute-start(f32[128,128]{0,1:T(8,128)S(1)} %add.129), channel_id=1, source_target_pairs={{0,128},{4,132},{8,136},{12,140},{16,144},{20,148},{24,152},{28,15... | collective-permute-start | bytes 196616 | tf_op jit(solution)/shard_map/ppermute | solution.py:14
  83.7 11.1 %copy-start.2 = (f32[128,128]{1,0:T(8,128)}, f32[128,128]{1,0:T(8,128)S(1)}, u32[]{:S(2)}) copy-start(f32[128,128]{1,0:T(8,128)S(1)} %fusion.8) | copy-start | bytes 196612
  94.8 4.5 %copy-start = (f32[128,16384]{1,0:T(8,128)}, f32[128,16384]{1,0:T(8,128)S(1)}, u32[]{:S(2)}) copy-start(f32[128,16384]{1,0:T(8,128)S(1)} %fusion.12) | copy-start | bytes 25165828
  99.3 7.5 %collective-permute-start.8 = (f32[64,16384]{1,0:T(8,128)}, f32[64,16384]{1,0:T(8,128)}, u32[]{:S(2)}, u32[]{:S(2)}) collective-permute-start(f32[64,16384]{1,0:T(8,128)} %constant_dynamic-slice_fusion.5), channel_id=1, source_target_pairs={{0,4},{4,0},{8,12},{12,8},{16,20},{20,16},{24,28},{28,24},{32,36},... | collective-permute-start | bytes 12582920 | tf_op jit(solution)/shard_map/ppermute | solution.py:35
  110.7 2.0 copy-start.1
  112.8 48.1 %collective-permute-start.9 = (f32[32,16384]{1,0:T(8,128)S(1)}, f32[32,16384]{1,0:T(8,128)}, u32[]{:S(2)}, u32[]{:S(2)}) collective-permute-start(f32[32,16384]{1,0:T(8,128)S(1)} %constant_dynamic-slice_fusion.4), channel_id=1, source_target_pairs={{0,8},{4,12},{8,0},{12,4},{16,24},{20,28},{24,16},{28,20},{32,40},... | collective-permute-start | bytes 6291464 | tf_op jit(solution)/shard_map/ppermute | solution.py:35
  163.3 80.1 %copy-start.4 = (f32[16,128]{1,0:T(8,128)S(1)}, f32[16,128]{1,0:T(8,128)}, u32[]{:S(2)}) copy-start(f32[16,128]{1,0:T(8,128)} %param.15) | copy-start | bytes 24580
  163.3 80.1 %copy-start.5 = (f32[8,128]{1,0:T(8,128)S(1)}, f32[8,128]{1,0:T(8,128)}, u32[]{:S(2)}) copy-start(f32[8,128]{1,0:T(8,128)} %param.16) | copy-start | bytes 12292
  163.4 87.8 %copy-start.3 = (f32[16,128]{1,0:T(8,128)S(1)}, f32[16,128]{1,0:T(8,128)}, u32[]{:S(2)}) copy-start(f32[16,128]{1,0:T(8,128)} %param.17) | copy-start | bytes 24580
  163.4 47.9 %collective-permute-start.10 = (f32[16,16384]{1,0:T(8,128)S(1)}, f32[16,16384]{1,0:T(8,128)}, u32[]{:S(2)}, u32[]{:S(2)}) collective-permute-start(f32[16,16384]{1,0:T(8,128)S(1)} %constant_dynamic-slice_fusion.3), channel_id=1, source_target_pairs={{0,16},{4,20},{8,24},{12,28},{16,0},{20,4},{24,8},{28,12},{32,48},... | collective-permute-start | bytes 3145736 | tf_op jit(solution)/shard_map/ppermute | solution.py:35
  212.7 29.3 %collective-permute-start.11 = (f32[8,16384]{1,0:T(8,128)S(1)}, f32[8,16384]{1,0:T(8,128)S(1)}, u32[]{:S(2)}, u32[]{:S(2)}) collective-permute-start(f32[8,16384]{1,0:T(8,128)S(1)} %constant_dynamic-slice_fusion.2), channel_id=1, source_target_pairs={{0,32},{4,36},{8,40},{12,44},{16,48},{20,52},{24,56},{28,60},{32,0... | collective-permute-start | bytes 1572872 | tf_op jit(solution)/shard_map/ppermute | solution.py:35
  242.1 7.4 %collective-permute-start.12 = (f32[4,16384]{1,0:T(4,128)S(1)}, f32[4,16384]{1,0:T(4,128)S(1)}, u32[]{:S(2)}, u32[]{:S(2)}) collective-permute-start(f32[4,16384]{1,0:T(4,128)S(1)} %constant_dynamic-slice_fusion.1), channel_id=1, source_target_pairs={{0,64},{4,68},{8,72},{12,76},{16,80},{20,84},{24,88},{28,92},{32,9... | collective-permute-start | bytes 786440 | tf_op jit(solution)/shard_map/ppermute | solution.py:35
  249.7 6.6 %collective-permute-start.13 = (f32[2,16384]{1,0:T(2,128)S(1)}, f32[2,16384]{1,0:T(2,128)S(1)}, u32[]{:S(2)}, u32[]{:S(2)}) collective-permute-start(f32[2,16384]{1,0:T(2,128)S(1)} %constant_dynamic-slice_fusion), channel_id=1, source_target_pairs={{0,128},{4,132},{8,136},{12,140},{16,144},{20,148},{24,152},{28,15... | collective-permute-start | bytes 393224 | tf_op jit(solution)/shard_map/ppermute | solution.py:35
  257.1 5.2 %collective-permute-start.14 = (f32[16,128]{1,0:T(8,128)S(1)}, f32[16,128]{1,0:T(8,128)S(1)}, u32[]{:S(2)}, u32[]{:S(2)}) collective-permute-start(f32[16,128]{1,0:T(8,128)S(1)} %fusion.13), channel_id=1, source_target_pairs={{0,1},{1,0},{2,3},{3,2},{4,5},{5,4},{6,7},{7,6},{8,9},{9,8},{10,11... | collective-permute-start | bytes 24584 | tf_op jit(solution)/shard_map/ppermute | solution.py:14

commit v2 on v1

--- a/solution.py
+++ b/solution.py
@@ -11,29 +11,46 @@
 def butterfly_sum(x, axis, size):
     step = 1
     while step < size:
-        x = x + lax.ppermute(x, axis, [(i, i ^ step) for i in range(size)])
-        step *= 2
+        if step * 4 <= size:
+            near = lax.ppermute(x, axis, [(i, i ^ step) for i in range(size)])
+            far = lax.ppermute(x, axis, [(i, i ^ (2 * step)) for i in range(size)])
+            farther = lax.ppermute(x, axis, [(i, i ^ (3 * step)) for i in range(size)])
+            x = (x + near) + (far + farther)
+            step *= 4
+        else:
+            x = x + lax.ppermute(x, axis, [(i, i ^ step) for i in range(size)])
+            step *= 2
     return x
 
 
-def bit_reverse(value, bits):
-    out = 0
-    for _ in range(bits):
-        out = (out << 1) | (value & 1)
-        value >>= 1
-    return out
+def scatter_steps(size):
+    if size == 64:
+        return {0: (1, 2, 16, 4, 32, 8), 1: (1, 16, 2, 32, 4, 8)}
+    plain = tuple(1 << k for k in range(size.bit_length() - 1))
+    return {0: plain, 1: plain}
+
+
+def scatter_layout(size, per):
+    steps = scatter_steps(size)
+    rounds = len(steps[0])
+    table = np.zeros((size, size * per), np.int32)
+    for d in range(size):
+        for b in range(size):
+            seq = steps[b & 1]
+            pos = 0
+            for r, st in enumerate(seq):
+                pos |= (((b ^ d) // st) % 2) << (rounds - 1 - r)
+            for t in range(per):
+                table[d, pos * per + t] = b * per + t
+    return table
 
 
 def halving_scatter(x, axis, size):
-    idx = lax.axis_index(axis)
-    step = 1
-    while step < size:
+    steps = scatter_steps(size)
+    for r in range(len(steps[0])):
         half = x.shape[0] // 2
-        bit = (idx // step) % 2
-        keep = lax.dynamic_slice_in_dim(x, bit * half, half, 0)
-        send = lax.dynamic_slice_in_dim(x, (1 - bit) * half, half, 0)
-        x = keep + lax.ppermute(send, axis, [(i, i ^ step) for i in range(size)])
-        step *= 2
+        perm = [(i, i ^ steps[i & 1][r]) for i in range(size)]
+        x = x[:half] + lax.ppermute(x[half:], axis, perm)
     return x
 
 
@@ -51,7 +68,7 @@
         * g_fourth[None, None, None, :, :]
     ).reshape(width, RANK)
     partial_sketch = jnp.dot(flat, omega, precision=highest, preferred_element_type=jnp.float32)
-    sketch = butterfly_sum(butterfly_sum(partial_sketch, "pa", n_pa), "pb", n_pb)
+    sketch = butterfly_sum(partial_sketch, ("pa", "pb"), n_pa * n_pb)
     gram = butterfly_sum(
         jnp.dot(sketch.T, sketch, precision=highest, preferred_element_type=jnp.float32), "space", n_space
     )
@@ -59,12 +76,11 @@
     basis = lax.linalg.triangular_solve(
         lower, sketch, left_side=False, lower=True, transpose_a=True
     )
-    bits = n_space.bit_length() - 1
     per = RANK // n_space
-    order = np.array([per * bit_reverse(b, bits) + t for b in range(n_space) for t in range(per)])
+    order = jnp.asarray(scatter_layout(n_space, per))[lax.axis_index("space")]
     core_flat = halving_scatter(
         lax.dot_general(
-            basis[:, order],
+            jnp.take(basis, order, axis=1),
             flat,
             (((0,), (0,)), ((), ())),
             precision=highest,

time: 264 us -> 187 us (0.71)
  waiting for transfers between devices: 157 us -> 99.4 us
  starting transfers between devices: 34.9 us -> 28.7 us
  local copies, waits for them, and re-layouts: 9.15 us -> 2.98 us
  other arithmetic: 33 us -> 27.4 us
    ppermute x6 -> x18, waiting for transfers between devices: 135 us -> 96.4 us  [the longest x6 78.3 us: halving_scatter(): x = x[:half] + lax.ppermute(x[half:], axis, perm)]
    ppermute x9 -> x1, starting transfers between devices: 22.9 us -> 0.88 us  [butterfly_sum(): x = x + lax.ppermute(x, axis, [(i, i ^ step) for i in range(size)])]
    ppermute x9 -> x1, waiting for transfers between devices: 22.8 us -> 2.99 us  [butterfly_sum(): x = x + lax.ppermute(x, axis, [(i, i ^ step) for i in range(size)])]
    ppermute x6 -> x18, starting transfers between devices: 11.9 us -> 27.9 us  [the longest x6 9.77 us: halving_scatter(): x = x[:half] + lax.ppermute(x[half:], axis, perm)]
    add x14 -> x10, other arithmetic: 7.93 us -> 1.02 us  [the longest x6 0.96 us: halving_scatter(): x = x[:half] + lax.ppermute(x[half:], axis, perm)]
    unnamed x14 -> x8, local copies, waits for them, and re-layouts: 4 us -> 0.03 us
    dynamic_slice x6 -> x0, local copies, waits for them, and re-layouts: 2.84 us -> none  [halving_scatter(): send = lax.dynamic_slice_in_dim(x, (1 - bit) * half, half, 0)]
  transfers between devices with their start and end apart: 15 -> 19, of which waited for: 15 -> 17; matrix products, arithmetic and copies ran while one was open for 1% -> 2% of each run, Pallas kernels for 0% -> 0%
where the time goes in v2:
time: 187 us
  waiting for transfers between devices  99.4 us (53%)
  starting transfers between devices  28.7 us (15%)
  other arithmetic  27.4 us (15%)
  matrix products  27.3 us (15%)
  local copies, waits for them, and re-layouts  2.98 us (2%)
    ppermute x6, waiting for transfers between devices, halving_scatter(): x = x[:half] + lax.ppermute(x[half:], axis, perm)  78.3 us
    dot_general x1, matrix products, body(): jnp.dot(flat, omega, precision=highest, preferred_element_type=jnp.float32)  16.1 us
    another operation x3, other arithmetic, body(): lower = jnp.linalg.cholesky(gram)  12.4 us
    another operation x2, other arithmetic, body(): lax.linalg.triangular_solve(lower, sketch, left_side=False, lower=True, t...  10.5 us
    dot_general x1, matrix products, body(): lax.dot_general(jnp.take(basis, order, axis=1), flat, (((0,), (0,)), ((),...  10 us
    ppermute x6, starting transfers between devices, halving_scatter(): x = x[:half] + lax.ppermute(x[half:], axis, perm)  9.77 us
    ppermute x4, waiting for transfers between devices, butterfly_sum(): far = lax.ppermute(x, axis, [(i, i ^ 2 * step) for i in range(size)])  9.09 us
    ppermute x4, starting transfers between devices, butterfly_sum(): far = lax.ppermute(x, axis, [(i, i ^ 2 * step) for i in range(size)])  8.72 us
  transfers between devices with their start and end apart: 19, of which 17 were waited for; matrix products, arithmetic and copies ran while one was open for 2% of the time, Pallas kernels for 0%

profile of v2, /device:TPU:24, one launch (start us, length us, event | category | flops | bytes accessed | tf_op | source)
XLA Modules:
  0.0 186.8 jit_solution(7983584966829880162)
XLA Ops:
  2.1 16.1 %fusion.4 = f32[128,128]{0,1:T(8,128)S(1)} fusion(f32[128,8,16,8,16]{0,4,3,2,1:T(8,128)} %param.9, f32[16,128]{1,0:T(8,128)} %param.13, f32[8,16,8,128]{3,2,1,0:T(8,128)S(1)} %broadcast_multiply_fusion.1), kind=kOutput, calls=%fused_computation.7 | convolution fusion | flops 3223322624 | bytes 8986624 | tf_op jit(solution)/shard_map/dot_general | solution.py:70
  18.2 3.1 %collective-permute-start = (f32[128,128]{0,1:T(8,128)S(1)}, f32[128,128]{0,1:T(8,128)S(1)}, u32[]{:S(2)}, u32[]{:S(2)}) collective-permute-start(f32[128,128]{0,1:T(8,128)S(1)} %fusion.4), channel_id=1, source_target_pairs={{0,1},{1,0},{2,3},{3,2},{4,5},{5,4},{6,7},{7,6},{8,9},{9,8},{10,11... | collective-permute-start | bytes 196616 | tf_op jit(solution)/shard_map/ppermute | solution.py:15
  25.6 1.8 collective-permute-done.2
  27.7 2.0 %collective-permute-start.4 = (f32[128,128]{0,1:T(8,128)S(1)}, f32[128,128]{0,1:T(8,128)S(1)}, u32[]{:S(2)}, u32[]{:S(2)}) collective-permute-start(f32[128,128]{0,1:T(8,128)S(1)} %fusion.17), channel_id=1, source_target_pairs={{0,8},{4,12},{8,0},{12,4},{16,24},{20,28},{24,16},{28,20},{32,40},... | collective-permute-start | bytes 196616 | tf_op jit(solution)/shard_map/ppermute | solution.py:16
  30.5 1.9 %collective-permute-done.4 = f32[128,128]{0,1:T(8,128)S(1)} collective-permute-done((f32[128,128]{0,1:T(8,128)S(1)}, f32[128,128]{0,1:T(8,128)S(1)}, u32[]{:S(2)}, u32[]{:S(2)}) %collective-permute-start.4) | collective-permute-done | bytes 65568 | tf_op jit(solution)/shard_map/ppermute | solution.py:16
  33.9 3.4 %collective-permute-start.6 = (f32[128,128]{0,1:T(8,128)S(1)}, f32[128,128]{0,1:T(8,128)S(1)}, u32[]{:S(2)}, u32[]{:S(2)}) collective-permute-start(f32[128,128]{0,1:T(8,128)S(1)} %add_add_fusion.2), channel_id=1, source_target_pairs={{0,16},{4,20},{8,24},{12,28},{16,0},{20,4},{24,8},{28,12},{32,48},... | collective-permute-start | bytes 196616 | tf_op jit(solution)/shard_map/ppermute | solution.py:15
  37.2 4.8 %collective-permute-start.7 = (f32[128,128]{0,1:T(8,128)S(1)}, f32[128,128]{0,1:T(8,128)S(1)}, u32[]{:S(2)}, u32[]{:S(2)}) collective-permute-start(f32[128,128]{0,1:T(8,128)S(1)} %add_add_fusion.2), channel_id=1, source_target_pairs={{0,32},{4,36},{8,40},{12,44},{16,48},{20,52},{24,56},{28,60},{32,0... | collective-permute-start | bytes 196616 | tf_op jit(solution)/shard_map/ppermute | solution.py:16
  42.0 3.7 %collective-permute-done.7 = f32[128,128]{0,1:T(8,128)S(1)} collective-permute-done((f32[128,128]{0,1:T(8,128)S(1)}, f32[128,128]{0,1:T(8,128)S(1)}, u32[]{:S(2)}, u32[]{:S(2)}) %collective-permute-start.7) | collective-permute-done | bytes 65568 | tf_op jit(solution)/shard_map/ppermute | solution.py:16
  45.7 2.7 %collective-permute-done.8 = f32[128,128]{0,1:T(8,128)S(1)} collective-permute-done((f32[128,128]{0,1:T(8,128)S(1)}, f32[128,128]{0,1:T(8,128)S(1)}, u32[]{:S(2)}, u32[]{:S(2)}) %collective-permute-start.8) | collective-permute-done | bytes 65568 | tf_op jit(solution)/shard_map/ppermute | solution.py:17
  49.7 2.2 %collective-permute-start.11 = (f32[128,128]{0,1:T(8,128)S(1)}, f32[128,128]{0,1:T(8,128)S(1)}, u32[]{:S(2)}, u32[]{:S(2)}) collective-permute-start(f32[128,128]{0,1:T(8,128)S(1)} %add_add_fusion.1), channel_id=1, source_target_pairs={{0,192},{4,196},{8,200},{12,204},{16,208},{20,212},{24,216},{28,22... | collective-permute-start | bytes 196616 | tf_op jit(solution)/shard_map/ppermute | solution.py:17
  52.7 2.0 %collective-permute-done.10 = f32[128,128]{0,1:T(8,128)S(1)} collective-permute-done((f32[128,128]{0,1:T(8,128)S(1)}, f32[128,128]{0,1:T(8,128)S(1)}, u32[]{:S(2)}, u32[]{:S(2)}) %collective-permute-start.10) | collective-permute-done | bytes 65568 | tf_op jit(solution)/shard_map/ppermute | solution.py:16
  56.3 11.7 %cholesky.16 = f32[128,128]{1,0:T(8,128)S(1)} custom-call(f32[128,128]{1,0:T(8,128)S(1)} %fusion.10), custom_call_target="Cholesky" | custom-call | tf_op jit(solution)/shard_map/jit(cholesky)/cholesky | solution.py:75
  69.4 9.8 %custom-call.6 = f32[1,128,128]{1,2,0:T(8,128)S(1)} custom-call(f32[1,128,128]{2,1,0:T(8,128)S(1)} %fusion.7), custom_call_target="InvertDiagBlocksLowerTriangular" | custom-call | tf_op jit(solution)/shard_map/triangular_solve | solution.py:76
  80.2 10.0 %fusion.11 = f32[128,16384]{1,0:T(8,128)S(1)} fusion(f32[128,16384]{0,1:T(8,128)} %bitcast.32, f32[128,128]{1,0:T(8,128)S(1)} %gather_fusion, pred[128]{0:T(512)(128)(4,1)S(1)} %compare_and_fusion), kind=kOutput, calls=%fused_computation.20 | convolution fusion | flops 3221241856 | bytes 16842880 | tf_op jit(solution)/shard_map/dot_general | solution.py:82
  90.6 7.1 %collective-permute-done.12 = f32[64,16384]{1,0:T(8,128)S(1)} collective-permute-done((f32[64,16384]{1,0:T(8,128)S(1)}, f32[64,16384]{1,0:T(8,128)S(1)}, u32[]{:S(2)}, u32[]{:S(2)}) %collective-permute-start.12) | collective-permute-done | bytes 4194336 | tf_op jit(solution)/shard_map/ppermute | solution.py:53
  98.4 2.1 %collective-permute-start.13 = (f32[32,16384]{1,0:T(8,128)S(1)}, f32[32,16384]{1,0:T(8,128)S(1)}, u32[]{:S(2)}, u32[]{:S(2)}) collective-permute-start(f32[32,16384]{1,0:T(8,128)S(1)} %slice.63), channel_id=1, source_target_pairs={{0,8},{4,68},{8,0},{12,76},{16,24},{20,84},{24,16},{28,92},{32,40}... | collective-permute-start | bytes 6291464 | tf_op jit(solution)/shard_map/ppermute | solution.py:53
  100.5 24.2 %collective-permute-done.13 = f32[32,16384]{1,0:T(8,128)S(1)} collective-permute-done((f32[32,16384]{1,0:T(8,128)S(1)}, f32[32,16384]{1,0:T(8,128)S(1)}, u32[]{:S(2)}, u32[]{:S(2)}) %collective-permute-start.13) | collective-permute-done | bytes 2097184 | tf_op jit(solution)/shard_map/ppermute | solution.py:53
  125.2 14.7 %collective-permute-done.14 = f32[16,16384]{1,0:T(8,128)S(1)} collective-permute-done((f32[16,16384]{1,0:T(8,128)S(1)}, f32[16,16384]{1,0:T(8,128)S(1)}, u32[]{:S(2)}, u32[]{:S(2)}) %collective-permute-start.14) | collective-permute-done | bytes 1048608 | tf_op jit(solution)/shard_map/ppermute | solution.py:53
  140.1 2.5 %collective-permute-start.15 = (f32[8,16384]{1,0:T(8,128)S(1)}, f32[8,16384]{1,0:T(8,128)S(1)}, u32[]{:S(2)}, u32[]{:S(2)}) collective-permute-start(f32[8,16384]{1,0:T(8,128)S(1)} %slice.67), channel_id=1, source_target_pairs={{0,16},{4,132},{8,24},{12,140},{16,0},{20,148},{24,8},{28,156},{32... | collective-permute-start | bytes 1572872 | tf_op jit(solution)/shard_map/ppermute | solution.py:53
  142.6 18.9 %collective-permute-done.15 = f32[8,16384]{1,0:T(8,128)S(1)} collective-permute-done((f32[8,16384]{1,0:T(8,128)S(1)}, f32[8,16384]{1,0:T(8,128)S(1)}, u32[]{:S(2)}, u32[]{:S(2)}) %collective-permute-start.15) | collective-permute-done | bytes 524320 | tf_op jit(solution)/shard_map/ppermute | solution.py:53
  162.4 7.2 %collective-permute-done.16 = f32[4,16384]{1,0:T(4,128)S(1)} collective-permute-done((f32[4,16384]{1,0:T(4,128)S(1)}, f32[4,16384]{1,0:T(4,128)S(1)}, u32[]{:S(2)}, u32[]{:S(2)}) %collective-permute-start.16) | collective-permute-done | bytes 262176 | tf_op jit(solution)/shard_map/ppermute | solution.py:53
  169.7 4.1 %collective-permute-start.17 = (f32[2,16384]{1,0:T(2,128)S(1)}, f32[2,16384]{1,0:T(2,128)S(1)}, u32[]{:S(2)}, u32[]{:S(2)}) collective-permute-start(f32[2,16384]{1,0:T(2,128)S(1)} %slice.71), channel_id=1, source_target_pairs={{0,32},{4,36},{8,40},{12,44},{16,48},{20,52},{24,56},{28,60},{32,0... | collective-permute-start | bytes 393224 | tf_op jit(solution)/shard_map/ppermute | solution.py:53
  174.0 6.1 %collective-permute-done.17 = f32[2,16384]{1,0:T(2,128)S(1)} collective-permute-done((f32[2,16384]{1,0:T(2,128)S(1)}, f32[2,16384]{1,0:T(2,128)S(1)}, u32[]{:S(2)}, u32[]{:S(2)}) %collective-permute-start.17) | collective-permute-done | bytes 131104 | tf_op jit(solution)/shard_map/ppermute | solution.py:53
  183.2 3.0 %collective-permute-done.18 = f32[16,128]{1,0:T(8,128)S(1)} collective-permute-done((f32[16,128]{1,0:T(8,128)S(1)}, f32[16,128]{1,0:T(8,128)S(1)}, u32[]{:S(2)}, u32[]{:S(2)}) %collective-permute-start.18) | collective-permute-done | bytes 8224 | tf_op jit(solution)/shard_map/ppermute | solution.py:21
  (62 shorter events, 20.7 us)
Async XLA Ops:
  18.2 5.9 %collective-permute-start = (f32[128,128]{0,1:T(8,128)S(1)}, f32[128,128]{0,1:T(8,128)S(1)}, u32[]{:S(2)}, u32[]{:S(2)}) collective-permute-start(f32[128,128]{0,1:T(8,128)S(1)} %fusion.4), channel_id=1, source_target_pairs={{0,1},{1,0},{2,3},{3,2},{4,5},{5,4},{6,7},{7,6},{8,9},{9,8},{10,11... | collective-permute-start | bytes 196616 | tf_op jit(solution)/shard_map/ppermute | solution.py:15
  21.3 4.3 %collective-permute-start.1 = (f32[128,128]{0,1:T(8,128)S(1)}, f32[128,128]{0,1:T(8,128)S(1)}, u32[]{:S(2)}, u32[]{:S(2)}) collective-permute-start(f32[128,128]{0,1:T(8,128)S(1)} %fusion.4), channel_id=1, source_target_pairs={{0,2},{1,3},{2,0},{3,1},{4,6},{5,7},{6,4},{7,5},{8,10},{9,11},{10,... | collective-permute-start | bytes 196616 | tf_op jit(solution)/shard_map/ppermute | solution.py:16
  21.9 5.5 %collective-permute-start.2 = (f32[128,128]{0,1:T(8,128)S(1)}, f32[128,128]{0,1:T(8,128)S(1)}, u32[]{:S(2)}, u32[]{:S(2)}) collective-permute-start(f32[128,128]{0,1:T(8,128)S(1)} %fusion.4), channel_id=1, source_target_pairs={{0,3},{1,2},{2,1},{3,0},{4,7},{5,6},{6,5},{7,4},{8,11},{9,10},{10,... | collective-permute-start | bytes 196616 | tf_op jit(solution)/shard_map/ppermute | solution.py:17
  27.6 2.8 %collective-permute-start.3 = (f32[128,128]{0,1:T(8,128)S(1)}, f32[128,128]{0,1:T(8,128)S(1)}, u32[]{:S(2)}, u32[]{:S(2)}) collective-permute-start(f32[128,128]{0,1:T(8,128)S(1)} %fusion.17), channel_id=1, source_target_pairs={{0,4},{4,0},{8,12},{12,8},{16,20},{20,16},{24,28},{28,24},{32,36},... | collective-permute-start | bytes 196616 | tf_op jit(solution)/shard_map/ppermute | solution.py:15
  27.7 4.7 %collective-permute-start.4 = (f32[128,128]{0,1:T(8,128)S(1)}, f32[128,128]{0,1:T(8,128)S(1)}, u32[]{:S(2)}, u32[]{:S(2)}) collective-permute-start(f32[128,128]{0,1:T(8,128)S(1)} %fusion.17), channel_id=1, source_target_pairs={{0,8},{4,12},{8,0},{12,4},{16,24},{20,28},{24,16},{28,20},{32,40},... | collective-permute-start | bytes 196616 | tf_op jit(solution)/shard_map/ppermute | solution.py:16
  29.8 4.1 %collective-permute-start.5 = (f32[128,128]{0,1:T(8,128)S(1)}, f32[128,128]{0,1:T(8,128)S(1)}, u32[]{:S(2)}, u32[]{:S(2)}) collective-permute-start(f32[128,128]{0,1:T(8,128)S(1)} %fusion.17), channel_id=1, source_target_pairs={{0,12},{4,8},{8,4},{12,0},{16,28},{20,24},{24,20},{28,16},{32,44},... | collective-permute-start | bytes 196616 | tf_op jit(solution)/shard_map/ppermute | solution.py:17
  33.9 8.2 %collective-permute-start.6 = (f32[128,128]{0,1:T(8,128)S(1)}, f32[128,128]{0,1:T(8,128)S(1)}, u32[]{:S(2)}, u32[]{:S(2)}) collective-permute-start(f32[128,128]{0,1:T(8,128)S(1)} %add_add_fusion.2), channel_id=1, source_target_pairs={{0,16},{4,20},{8,24},{12,28},{16,0},{20,4},{24,8},{28,12},{32,48},... | collective-permute-start | bytes 196616 | tf_op jit(solution)/shard_map/ppermute | solution.py:15
  37.2 8.5 %collective-permute-start.7 = (f32[128,128]{0,1:T(8,128)S(1)}, f32[128,128]{0,1:T(8,128)S(1)}, u32[]{:S(2)}, u32[]{:S(2)}) collective-permute-start(f32[128,128]{0,1:T(8,128)S(1)} %add_add_fusion.2), channel_id=1, source_target_pairs={{0,32},{4,36},{8,40},{12,44},{16,48},{20,52},{24,56},{28,60},{32,0... | collective-permute-start | bytes 196616 | tf_op jit(solution)/shard_map/ppermute | solution.py:16
  42.0 6.4 %collective-permute-start.8 = (f32[128,128]{0,1:T(8,128)S(1)}, f32[128,128]{0,1:T(8,128)S(1)}, u32[]{:S(2)}, u32[]{:S(2)}) collective-permute-start(f32[128,128]{0,1:T(8,128)S(1)} %add_add_fusion.2), channel_id=1, source_target_pairs={{0,48},{4,52},{8,56},{12,60},{16,32},{20,36},{24,40},{28,44},{32,1... | collective-permute-start | bytes 196616 | tf_op jit(solution)/shard_map/ppermute | solution.py:17
  48.4 6.2 %collective-permute-start.10 = (f32[128,128]{0,1:T(8,128)S(1)}, f32[128,128]{0,1:T(8,128)S(1)}, u32[]{:S(2)}, u32[]{:S(2)}) collective-permute-start(f32[128,128]{0,1:T(8,128)S(1)} %add_add_fusion.1), channel_id=1, source_target_pairs={{0,128},{4,132},{8,136},{12,140},{16,144},{20,148},{24,152},{28,15... | collective-permute-start | bytes 196616 | tf_op jit(solution)/shard_map/ppermute | solution.py:16
  49.7 5.6 %collective-permute-start.11 = (f32[128,128]{0,1:T(8,128)S(1)}, f32[128,128]{0,1:T(8,128)S(1)}, u32[]{:S(2)}, u32[]{:S(2)}) collective-permute-start(f32[128,128]{0,1:T(8,128)S(1)} %add_add_fusion.1), channel_id=1, source_target_pairs={{0,192},{4,196},{8,200},{12,204},{16,208},{20,212},{24,216},{28,22... | collective-permute-start | bytes 196616 | tf_op jit(solution)/shard_map/ppermute | solution.py:17
  51.9 4.3 %collective-permute-start.9 = (f32[128,128]{0,1:T(8,128)S(1)}, f32[128,128]{0,1:T(8,128)S(1)}, u32[]{:S(2)}, u32[]{:S(2)}) collective-permute-start(f32[128,128]{0,1:T(8,128)S(1)} %add_add_fusion.1), channel_id=1, source_target_pairs={{0,64},{4,68},{8,72},{12,76},{16,80},{20,84},{24,88},{28,92},{32,9... | collective-permute-start | bytes 196616 | tf_op jit(solution)/shard_map/ppermute | solution.py:15
  79.5 10.8 %copy-start = (f32[128,128]{1,0:T(8,128)}, f32[128,128]{1,0:T(8,128)S(1)}, u32[]{:S(2)}) copy-start(f32[128,128]{1,0:T(8,128)S(1)} %fusion.8) | copy-start | bytes 196612
  90.5 7.2 %collective-permute-start.12 = (f32[64,16384]{1,0:T(8,128)S(1)}, f32[64,16384]{1,0:T(8,128)S(1)}, u32[]{:S(2)}, u32[]{:S(2)}) collective-permute-start(f32[64,16384]{1,0:T(8,128)S(1)} %slice.61), channel_id=1, source_target_pairs={{0,4},{4,0},{8,12},{12,8},{16,20},{20,16},{24,28},{28,24},{32,36},... | collective-permute-start | bytes 12582920 | tf_op jit(solution)/shard_map/ppermute | solution.py:53
  98.3 64.0 %copy-start.2 = (f32[16,128]{1,0:T(8,128)S(1)}, f32[16,128]{1,0:T(8,128)}, u32[]{:S(2)}) copy-start(f32[16,128]{1,0:T(8,128)} %param.14) | copy-start | bytes 24580
  98.4 64.0 %copy-start.3 = (f32[8,128]{1,0:T(8,128)S(1)}, f32[8,128]{1,0:T(8,128)}, u32[]{:S(2)}) copy-start(f32[8,128]{1,0:T(8,128)} %param.15) | copy-start | bytes 12292
  98.4 75.5 %copy-start.1 = (f32[16,128]{1,0:T(8,128)S(1)}, f32[16,128]{1,0:T(8,128)}, u32[]{:S(2)}) copy-start(f32[16,128]{1,0:T(8,128)} %param.16) | copy-start | bytes 24580
  98.4 26.3 %collective-permute-start.13 = (f32[32,16384]{1,0:T(8,128)S(1)}, f32[32,16384]{1,0:T(8,128)S(1)}, u32[]{:S(2)}, u32[]{:S(2)}) collective-permute-start(f32[32,16384]{1,0:T(8,128)S(1)} %slice.63), channel_id=1, source_target_pairs={{0,8},{4,68},{8,0},{12,76},{16,24},{20,84},{24,16},{28,92},{32,40}... | collective-permute-start | bytes 6291464 | tf_op jit(solution)/shard_map/ppermute | solution.py:53
  125.0 14.9 %collective-permute-start.14 = (f32[16,16384]{1,0:T(8,128)S(1)}, f32[16,16384]{1,0:T(8,128)S(1)}, u32[]{:S(2)}, u32[]{:S(2)}) collective-permute-start(f32[16,16384]{1,0:T(8,128)S(1)} %slice.65), channel_id=1, source_target_pairs={{0,64},{4,12},{8,72},{12,4},{16,80},{20,28},{24,88},{28,20},{32,96... | collective-permute-start | bytes 3145736 | tf_op jit(solution)/shard_map/ppermute | solution.py:53
  140.1 21.4 %collective-permute-start.15 = (f32[8,16384]{1,0:T(8,128)S(1)}, f32[8,16384]{1,0:T(8,128)S(1)}, u32[]{:S(2)}, u32[]{:S(2)}) collective-permute-start(f32[8,16384]{1,0:T(8,128)S(1)} %slice.67), channel_id=1, source_target_pairs={{0,16},{4,132},{8,24},{12,140},{16,0},{20,148},{24,8},{28,156},{32... | collective-permute-start | bytes 1572872 | tf_op jit(solution)/shard_map/ppermute | solution.py:53
  161.6 8.0 %collective-permute-start.16 = (f32[4,16384]{1,0:T(4,128)S(1)}, f32[4,16384]{1,0:T(4,128)S(1)}, u32[]{:S(2)}, u32[]{:S(2)}) collective-permute-start(f32[4,16384]{1,0:T(4,128)S(1)} %slice.69), channel_id=1, source_target_pairs={{0,128},{4,20},{8,136},{12,28},{16,144},{20,4},{24,152},{28,12},{3... | collective-permute-start | bytes 786440 | tf_op jit(solution)/shard_map/ppermute | solution.py:53
  169.7 10.4 %collective-permute-start.17 = (f32[2,16384]{1,0:T(2,128)S(1)}, f32[2,16384]{1,0:T(2,128)S(1)}, u32[]{:S(2)}, u32[]{:S(2)}) collective-permute-start(f32[2,16384]{1,0:T(2,128)S(1)} %slice.71), channel_id=1, source_target_pairs={{0,32},{4,36},{8,40},{12,44},{16,48},{20,52},{24,56},{28,60},{32,0... | collective-permute-start | bytes 393224 | tf_op jit(solution)/shard_map/ppermute | solution.py:53
  180.9 5.2 %collective-permute-start.18 = (f32[16,128]{1,0:T(8,128)S(1)}, f32[16,128]{1,0:T(8,128)S(1)}, u32[]{:S(2)}, u32[]{:S(2)}) collective-permute-start(f32[16,128]{1,0:T(8,128)S(1)} %fusion.18), channel_id=1, source_target_pairs={{0,1},{1,0},{2,3},{3,2},{4,5},{5,4},{6,7},{7,6},{8,9},{9,8},{10,11... | collective-permute-start | bytes 24584 | tf_op jit(solution)/shard_map/ppermute | solution.py:21

commit v3 on v2

--- a/solution.py
+++ b/solution.py
@@ -67,7 +67,7 @@
         * g_third[None, None, :, None, :]
         * g_fourth[None, None, None, :, :]
     ).reshape(width, RANK)
-    partial_sketch = jnp.dot(flat, omega, precision=highest, preferred_element_type=jnp.float32)
+    partial_sketch = jnp.dot(flat, omega, precision=lax.Precision.HIGH, preferred_element_type=jnp.float32)
     sketch = butterfly_sum(partial_sketch, ("pa", "pb"), n_pa * n_pb)
     gram = butterfly_sum(
         jnp.dot(sketch.T, sketch, precision=highest, preferred_element_type=jnp.float32), "space", n_space
@@ -83,7 +83,7 @@
             jnp.take(basis, order, axis=1),
             flat,
             (((0,), (0,)), ((), ())),
-            precision=highest,
+            precision=lax.Precision.HIGH,
             preferred_element_type=jnp.float32,
         ),
         "space",

time: 187 us -> 176 us (0.941)
  matrix products: 27.3 us -> 16.7 us
    dot_general x1, matrix products: 16.1 us -> 9.15 us  [body(): jnp.dot(flat, omega, precision=lax.Precision.HIGH, preferred_element_type...]
    dot_general x1, matrix products: 10 us -> 6.34 us  [body(): lax.dot_general(jnp.take(basis, order, axis=1), flat, (((0,), (0,)), ((),...]
where the time goes in v3:
time: 176 us
  waiting for transfers between devices  99.4 us (56%)
  starting transfers between devices  28.8 us (16%)
  other arithmetic  27.4 us (16%)
  matrix products  16.7 us (9%)
  local copies, waits for them, and re-layouts  2.98 us (2%)
    ppermute x6, waiting for transfers between devices, halving_scatter(): x = x[:half] + lax.ppermute(x[half:], axis, perm)  78.3 us
    another operation x3, other arithmetic, body(): lower = jnp.linalg.cholesky(gram)  12.4 us
    another operation x2, other arithmetic, body(): lax.linalg.triangular_solve(lower, sketch, left_side=False, lower=True, t...  10.5 us
    ppermute x6, starting transfers between devices, halving_scatter(): x = x[:half] + lax.ppermute(x[half:], axis, perm)  9.77 us
    dot_general x1, matrix products, body(): jnp.dot(flat, omega, precision=lax.Precision.HIGH, preferred_element_type...  9.15 us
    ppermute x4, waiting for transfers between devices, butterfly_sum(): far = lax.ppermute(x, axis, [(i, i ^ 2 * step) for i in range(size)])  9.09 us
    ppermute x4, starting transfers between devices, butterfly_sum(): far = lax.ppermute(x, axis, [(i, i ^ 2 * step) for i in range(size)])  8.72 us
    ppermute x4, starting transfers between devices, butterfly_sum(): near = lax.ppermute(x, axis, [(i, i ^ step) for i in range(size)])  6.63 us
  transfers between devices with their start and end apart: 19, of which 17 were waited for; matrix products, arithmetic and copies ran while one was open for 2% of the time, Pallas kernels for 0%

profile of v3, /device:TPU:24, one launch (start us, length us, event | category | flops | bytes accessed | tf_op | source)
XLA Modules:
  0.0 176.1 jit_solution(1756273120419216549)
XLA Ops:
  2.1 9.1 %fusion.4 = f32[128,128]{0,1:T(8,128)S(1)} fusion(f32[128,8,16,8,16]{0,4,3,2,1:T(8,128)} %param.9, f32[16,128]{1,0:T(8,128)} %param.13, f32[8,16,8,128]{3,2,1,0:T(8,128)S(1)} %broadcast_multiply_fusion.1), kind=kOutput, calls=%fused_computation.7 | convolution fusion | flops 1612709888 | bytes 8986624 | tf_op jit(solution)/shard_map/dot_general | solution.py:70
  11.2 3.1 %collective-permute-start = (f32[128,128]{0,1:T(8,128)S(1)}, f32[128,128]{0,1:T(8,128)S(1)}, u32[]{:S(2)}, u32[]{:S(2)}) collective-permute-start(f32[128,128]{0,1:T(8,128)S(1)} %fusion.4), channel_id=1, source_target_pairs={{0,1},{1,0},{2,3},{3,2},{4,5},{5,4},{6,7},{7,6},{8,9},{9,8},{10,11... | collective-permute-start | bytes 196616 | tf_op jit(solution)/shard_map/ppermute | solution.py:15
  18.6 1.8 %collective-permute-done.2 = f32[128,128]{0,1:T(8,128)S(1)} collective-permute-done((f32[128,128]{0,1:T(8,128)S(1)}, f32[128,128]{0,1:T(8,128)S(1)}, u32[]{:S(2)}, u32[]{:S(2)}) %collective-permute-start.2) | collective-permute-done | bytes 65568 | tf_op jit(solution)/shard_map/ppermute | solution.py:17
  20.8 2.0 %collective-permute-start.4 = (f32[128,128]{0,1:T(8,128)S(1)}, f32[128,128]{0,1:T(8,128)S(1)}, u32[]{:S(2)}, u32[]{:S(2)}) collective-permute-start(f32[128,128]{0,1:T(8,128)S(1)} %fusion.17), channel_id=1, source_target_pairs={{0,8},{4,12},{8,0},{12,4},{16,24},{20,28},{24,16},{28,20},{32,40},... | collective-permute-start | bytes 196616 | tf_op jit(solution)/shard_map/ppermute | solution.py:16
  23.5 1.9 %collective-permute-done.4 = f32[128,128]{0,1:T(8,128)S(1)} collective-permute-done((f32[128,128]{0,1:T(8,128)S(1)}, f32[128,128]{0,1:T(8,128)S(1)}, u32[]{:S(2)}, u32[]{:S(2)}) %collective-permute-start.4) | collective-permute-done | bytes 65568 | tf_op jit(solution)/shard_map/ppermute | solution.py:16
  26.9 3.4 %collective-permute-start.6 = (f32[128,128]{0,1:T(8,128)S(1)}, f32[128,128]{0,1:T(8,128)S(1)}, u32[]{:S(2)}, u32[]{:S(2)}) collective-permute-start(f32[128,128]{0,1:T(8,128)S(1)} %add_add_fusion.2), channel_id=1, source_target_pairs={{0,16},{4,20},{8,24},{12,28},{16,0},{20,4},{24,8},{28,12},{32,48},... | collective-permute-start | bytes 196616 | tf_op jit(solution)/shard_map/ppermute | solution.py:15
  30.2 4.8 %collective-permute-start.7 = (f32[128,128]{0,1:T(8,128)S(1)}, f32[128,128]{0,1:T(8,128)S(1)}, u32[]{:S(2)}, u32[]{:S(2)}) collective-permute-start(f32[128,128]{0,1:T(8,128)S(1)} %add_add_fusion.2), channel_id=1, source_target_pairs={{0,32},{4,36},{8,40},{12,44},{16,48},{20,52},{24,56},{28,60},{32,0... | collective-permute-start | bytes 196616 | tf_op jit(solution)/shard_map/ppermute | solution.py:16
  35.1 3.7 %collective-permute-done.7 = f32[128,128]{0,1:T(8,128)S(1)} collective-permute-done((f32[128,128]{0,1:T(8,128)S(1)}, f32[128,128]{0,1:T(8,128)S(1)}, u32[]{:S(2)}, u32[]{:S(2)}) %collective-permute-start.7) | collective-permute-done | bytes 65568 | tf_op jit(solution)/shard_map/ppermute | solution.py:16
  38.8 2.7 %collective-permute-done.8 = f32[128,128]{0,1:T(8,128)S(1)} collective-permute-done((f32[128,128]{0,1:T(8,128)S(1)}, f32[128,128]{0,1:T(8,128)S(1)}, u32[]{:S(2)}, u32[]{:S(2)}) %collective-permute-start.8) | collective-permute-done | bytes 65568 | tf_op jit(solution)/shard_map/ppermute | solution.py:17
  42.8 2.2 %collective-permute-start.11 = (f32[128,128]{0,1:T(8,128)S(1)}, f32[128,128]{0,1:T(8,128)S(1)}, u32[]{:S(2)}, u32[]{:S(2)}) collective-permute-start(f32[128,128]{0,1:T(8,128)S(1)} %add_add_fusion.1), channel_id=1, source_target_pairs={{0,192},{4,196},{8,200},{12,204},{16,208},{20,212},{24,216},{28,22... | collective-permute-start | bytes 196616 | tf_op jit(solution)/shard_map/ppermute | solution.py:17
  45.7 2.0 %collective-permute-done.10 = f32[128,128]{0,1:T(8,128)S(1)} collective-permute-done((f32[128,128]{0,1:T(8,128)S(1)}, f32[128,128]{0,1:T(8,128)S(1)}, u32[]{:S(2)}, u32[]{:S(2)}) %collective-permute-start.10) | collective-permute-done | bytes 65568 | tf_op jit(solution)/shard_map/ppermute | solution.py:16
  49.4 11.7 %cholesky.16 = f32[128,128]{1,0:T(8,128)S(1)} custom-call(f32[128,128]{1,0:T(8,128)S(1)} %fusion.10), custom_call_target="Cholesky" | custom-call | tf_op jit(solution)/shard_map/jit(cholesky)/cholesky | solution.py:75
  62.4 9.8 %custom-call.6 = f32[1,128,128]{1,2,0:T(8,128)S(1)} custom-call(f32[1,128,128]{2,1,0:T(8,128)S(1)} %fusion.7), custom_call_target="InvertDiagBlocksLowerTriangular" | custom-call | tf_op jit(solution)/shard_map/triangular_solve | solution.py:76
  73.3 6.3 %fusion.11 = f32[128,16384]{1,0:T(8,128)S(1)} fusion(f32[128,16384]{0,1:T(8,128)} %bitcast.32, f32[128,128]{1,0:T(8,128)S(1)} %gather_fusion, pred[128]{0:T(512)(128)(4,1)S(1)} %compare_and_fusion), kind=kOutput, calls=%fused_computation.20 | convolution fusion | flops 1610629120 | bytes 16842880 | tf_op jit(solution)/shard_map/dot_general | solution.py:82
  80.0 7.1 %collective-permute-done.12 = f32[64,16384]{1,0:T(8,128)S(1)} collective-permute-done((f32[64,16384]{1,0:T(8,128)S(1)}, f32[64,16384]{1,0:T(8,128)S(1)}, u32[]{:S(2)}, u32[]{:S(2)}) %collective-permute-start.12) | collective-permute-done | bytes 4194336 | tf_op jit(solution)/shard_map/ppermute | solution.py:53
  87.8 1.9 %collective-permute-start.13 = (f32[32,16384]{1,0:T(8,128)S(1)}, f32[32,16384]{1,0:T(8,128)S(1)}, u32[]{:S(2)}, u32[]{:S(2)}) collective-permute-start(f32[32,16384]{1,0:T(8,128)S(1)} %slice.63), channel_id=1, source_target_pairs={{0,8},{4,68},{8,0},{12,76},{16,24},{20,84},{24,16},{28,92},{32,40}... | collective-permute-start | bytes 6291464 | tf_op jit(solution)/shard_map/ppermute | solution.py:53
  89.7 24.2 %collective-permute-done.13 = f32[32,16384]{1,0:T(8,128)S(1)} collective-permute-done((f32[32,16384]{1,0:T(8,128)S(1)}, f32[32,16384]{1,0:T(8,128)S(1)}, u32[]{:S(2)}, u32[]{:S(2)}) %collective-permute-start.13) | collective-permute-done | bytes 2097184 | tf_op jit(solution)/shard_map/ppermute | solution.py:53
  114.3 14.7 %collective-permute-done.14 = f32[16,16384]{1,0:T(8,128)S(1)} collective-permute-done((f32[16,16384]{1,0:T(8,128)S(1)}, f32[16,16384]{1,0:T(8,128)S(1)}, u32[]{:S(2)}, u32[]{:S(2)}) %collective-permute-start.14) | collective-permute-done | bytes 1048608 | tf_op jit(solution)/shard_map/ppermute | solution.py:53
  129.2 2.5 %collective-permute-start.15 = (f32[8,16384]{1,0:T(8,128)S(1)}, f32[8,16384]{1,0:T(8,128)S(1)}, u32[]{:S(2)}, u32[]{:S(2)}) collective-permute-start(f32[8,16384]{1,0:T(8,128)S(1)} %slice.67), channel_id=1, source_target_pairs={{0,16},{4,132},{8,24},{12,140},{16,0},{20,148},{24,8},{28,156},{32... | collective-permute-start | bytes 1572872 | tf_op jit(solution)/shard_map/ppermute | solution.py:53
  131.7 18.9 %collective-permute-done.15 = f32[8,16384]{1,0:T(8,128)S(1)} collective-permute-done((f32[8,16384]{1,0:T(8,128)S(1)}, f32[8,16384]{1,0:T(8,128)S(1)}, u32[]{:S(2)}, u32[]{:S(2)}) %collective-permute-start.15) | collective-permute-done | bytes 524320 | tf_op jit(solution)/shard_map/ppermute | solution.py:53
  151.7 7.2 %collective-permute-done.16 = f32[4,16384]{1,0:T(4,128)S(1)} collective-permute-done((f32[4,16384]{1,0:T(4,128)S(1)}, f32[4,16384]{1,0:T(4,128)S(1)}, u32[]{:S(2)}, u32[]{:S(2)}) %collective-permute-start.16) | collective-permute-done | bytes 262176 | tf_op jit(solution)/shard_map/ppermute | solution.py:53
  159.1 4.1 %collective-permute-start.17 = (f32[2,16384]{1,0:T(2,128)S(1)}, f32[2,16384]{1,0:T(2,128)S(1)}, u32[]{:S(2)}, u32[]{:S(2)}) collective-permute-start(f32[2,16384]{1,0:T(2,128)S(1)} %slice.71), channel_id=1, source_target_pairs={{0,32},{4,36},{8,40},{12,44},{16,48},{20,52},{24,56},{28,60},{32,0... | collective-permute-start | bytes 393224 | tf_op jit(solution)/shard_map/ppermute | solution.py:53
  163.4 6.1 %collective-permute-done.17 = f32[2,16384]{1,0:T(2,128)S(1)} collective-permute-done((f32[2,16384]{1,0:T(2,128)S(1)}, f32[2,16384]{1,0:T(2,128)S(1)}, u32[]{:S(2)}, u32[]{:S(2)}) %collective-permute-start.17) | collective-permute-done | bytes 131104 | tf_op jit(solution)/shard_map/ppermute | solution.py:53
  172.5 3.0 %collective-permute-done.18 = f32[16,128]{1,0:T(8,128)S(1)} collective-permute-done((f32[16,128]{1,0:T(8,128)S(1)}, f32[16,128]{1,0:T(8,128)S(1)}, u32[]{:S(2)}, u32[]{:S(2)}) %collective-permute-start.18) | collective-permute-done | bytes 8224 | tf_op jit(solution)/shard_map/ppermute | solution.py:21
  (62 shorter events, 20.9 us)
Async XLA Ops:
  11.2 5.9 %collective-permute-start = (f32[128,128]{0,1:T(8,128)S(1)}, f32[128,128]{0,1:T(8,128)S(1)}, u32[]{:S(2)}, u32[]{:S(2)}) collective-permute-start(f32[128,128]{0,1:T(8,128)S(1)} %fusion.4), channel_id=1, source_target_pairs={{0,1},{1,0},{2,3},{3,2},{4,5},{5,4},{6,7},{7,6},{8,9},{9,8},{10,11... | collective-permute-start | bytes 196616 | tf_op jit(solution)/shard_map/ppermute | solution.py:15
  14.3 4.3 %collective-permute-start.1 = (f32[128,128]{0,1:T(8,128)S(1)}, f32[128,128]{0,1:T(8,128)S(1)}, u32[]{:S(2)}, u32[]{:S(2)}) collective-permute-start(f32[128,128]{0,1:T(8,128)S(1)} %fusion.4), channel_id=1, source_target_pairs={{0,2},{1,3},{2,0},{3,1},{4,6},{5,7},{6,4},{7,5},{8,10},{9,11},{10,... | collective-permute-start | bytes 196616 | tf_op jit(solution)/shard_map/ppermute | solution.py:16
  14.9 5.5 %collective-permute-start.2 = (f32[128,128]{0,1:T(8,128)S(1)}, f32[128,128]{0,1:T(8,128)S(1)}, u32[]{:S(2)}, u32[]{:S(2)}) collective-permute-start(f32[128,128]{0,1:T(8,128)S(1)} %fusion.4), channel_id=1, source_target_pairs={{0,3},{1,2},{2,1},{3,0},{4,7},{5,6},{6,5},{7,4},{8,11},{9,10},{10,... | collective-permute-start | bytes 196616 | tf_op jit(solution)/shard_map/ppermute | solution.py:17
  20.7 2.8 %collective-permute-start.3 = (f32[128,128]{0,1:T(8,128)S(1)}, f32[128,128]{0,1:T(8,128)S(1)}, u32[]{:S(2)}, u32[]{:S(2)}) collective-permute-start(f32[128,128]{0,1:T(8,128)S(1)} %fusion.17), channel_id=1, source_target_pairs={{0,4},{4,0},{8,12},{12,8},{16,20},{20,16},{24,28},{28,24},{32,36},... | collective-permute-start | bytes 196616 | tf_op jit(solution)/shard_map/ppermute | solution.py:15
  20.8 4.7 %collective-permute-start.4 = (f32[128,128]{0,1:T(8,128)S(1)}, f32[128,128]{0,1:T(8,128)S(1)}, u32[]{:S(2)}, u32[]{:S(2)}) collective-permute-start(f32[128,128]{0,1:T(8,128)S(1)} %fusion.17), channel_id=1, source_target_pairs={{0,8},{4,12},{8,0},{12,4},{16,24},{20,28},{24,16},{28,20},{32,40},... | collective-permute-start | bytes 196616 | tf_op jit(solution)/shard_map/ppermute | solution.py:16
  22.8 4.1 %collective-permute-start.5 = (f32[128,128]{0,1:T(8,128)S(1)}, f32[128,128]{0,1:T(8,128)S(1)}, u32[]{:S(2)}, u32[]{:S(2)}) collective-permute-start(f32[128,128]{0,1:T(8,128)S(1)} %fusion.17), channel_id=1, source_target_pairs={{0,12},{4,8},{8,4},{12,0},{16,28},{20,24},{24,20},{28,16},{32,44},... | collective-permute-start | bytes 196616 | tf_op jit(solution)/shard_map/ppermute | solution.py:17
  26.9 8.2 %collective-permute-start.6 = (f32[128,128]{0,1:T(8,128)S(1)}, f32[128,128]{0,1:T(8,128)S(1)}, u32[]{:S(2)}, u32[]{:S(2)}) collective-permute-start(f32[128,128]{0,1:T(8,128)S(1)} %add_add_fusion.2), channel_id=1, source_target_pairs={{0,16},{4,20},{8,24},{12,28},{16,0},{20,4},{24,8},{28,12},{32,48},... | collective-permute-start | bytes 196616 | tf_op jit(solution)/shard_map/ppermute | solution.py:15
  30.2 8.5 %collective-permute-start.7 = (f32[128,128]{0,1:T(8,128)S(1)}, f32[128,128]{0,1:T(8,128)S(1)}, u32[]{:S(2)}, u32[]{:S(2)}) collective-permute-start(f32[128,128]{0,1:T(8,128)S(1)} %add_add_fusion.2), channel_id=1, source_target_pairs={{0,32},{4,36},{8,40},{12,44},{16,48},{20,52},{24,56},{28,60},{32,0... | collective-permute-start | bytes 196616 | tf_op jit(solution)/shard_map/ppermute | solution.py:16
  35.0 6.4 %collective-permute-start.8 = (f32[128,128]{0,1:T(8,128)S(1)}, f32[128,128]{0,1:T(8,128)S(1)}, u32[]{:S(2)}, u32[]{:S(2)}) collective-permute-start(f32[128,128]{0,1:T(8,128)S(1)} %add_add_fusion.2), channel_id=1, source_target_pairs={{0,48},{4,52},{8,56},{12,60},{16,32},{20,36},{24,40},{28,44},{32,1... | collective-permute-start | bytes 196616 | tf_op jit(solution)/shard_map/ppermute | solution.py:17
  41.4 6.2 %collective-permute-start.10 = (f32[128,128]{0,1:T(8,128)S(1)}, f32[128,128]{0,1:T(8,128)S(1)}, u32[]{:S(2)}, u32[]{:S(2)}) collective-permute-start(f32[128,128]{0,1:T(8,128)S(1)} %add_add_fusion.1), channel_id=1, source_target_pairs={{0,128},{4,132},{8,136},{12,140},{16,144},{20,148},{24,152},{28,15... | collective-permute-start | bytes 196616 | tf_op jit(solution)/shard_map/ppermute | solution.py:16
  42.8 5.6 %collective-permute-start.11 = (f32[128,128]{0,1:T(8,128)S(1)}, f32[128,128]{0,1:T(8,128)S(1)}, u32[]{:S(2)}, u32[]{:S(2)}) collective-permute-start(f32[128,128]{0,1:T(8,128)S(1)} %add_add_fusion.1), channel_id=1, source_target_pairs={{0,192},{4,196},{8,200},{12,204},{16,208},{20,212},{24,216},{28,22... | collective-permute-start | bytes 196616 | tf_op jit(solution)/shard_map/ppermute | solution.py:17
  44.9 4.3 %collective-permute-start.9 = (f32[128,128]{0,1:T(8,128)S(1)}, f32[128,128]{0,1:T(8,128)S(1)}, u32[]{:S(2)}, u32[]{:S(2)}) collective-permute-start(f32[128,128]{0,1:T(8,128)S(1)} %add_add_fusion.1), channel_id=1, source_target_pairs={{0,64},{4,68},{8,72},{12,76},{16,80},{20,84},{24,88},{28,92},{32,9... | collective-permute-start | bytes 196616 | tf_op jit(solution)/shard_map/ppermute | solution.py:15
  72.5 7.1 %copy-start = (f32[128,128]{1,0:T(8,128)}, f32[128,128]{1,0:T(8,128)S(1)}, u32[]{:S(2)}) copy-start(f32[128,128]{1,0:T(8,128)S(1)} %fusion.8) | copy-start | bytes 196612
  79.9 7.2 %collective-permute-start.12 = (f32[64,16384]{1,0:T(8,128)S(1)}, f32[64,16384]{1,0:T(8,128)S(1)}, u32[]{:S(2)}, u32[]{:S(2)}) collective-permute-start(f32[64,16384]{1,0:T(8,128)S(1)} %slice.61), channel_id=1, source_target_pairs={{0,4},{4,0},{8,12},{12,8},{16,20},{20,16},{24,28},{28,24},{32,36},... | collective-permute-start | bytes 12582920 | tf_op jit(solution)/shard_map/ppermute | solution.py:53
  87.7 64.0 %copy-start.2 = (f32[16,128]{1,0:T(8,128)S(1)}, f32[16,128]{1,0:T(8,128)}, u32[]{:S(2)}) copy-start(f32[16,128]{1,0:T(8,128)} %param.14) | copy-start | bytes 24580
  87.7 64.0 %copy-start.3 = (f32[8,128]{1,0:T(8,128)S(1)}, f32[8,128]{1,0:T(8,128)}, u32[]{:S(2)}) copy-start(f32[8,128]{1,0:T(8,128)} %param.15) | copy-start | bytes 12292
  87.7 75.5 %copy-start.1 = (f32[16,128]{1,0:T(8,128)S(1)}, f32[16,128]{1,0:T(8,128)}, u32[]{:S(2)}) copy-start(f32[16,128]{1,0:T(8,128)} %param.16) | copy-start | bytes 24580
  87.8 26.1 %collective-permute-start.13 = (f32[32,16384]{1,0:T(8,128)S(1)}, f32[32,16384]{1,0:T(8,128)S(1)}, u32[]{:S(2)}, u32[]{:S(2)}) collective-permute-start(f32[32,16384]{1,0:T(8,128)S(1)} %slice.63), channel_id=1, source_target_pairs={{0,8},{4,68},{8,0},{12,76},{16,24},{20,84},{24,16},{28,92},{32,40}... | collective-permute-start | bytes 6291464 | tf_op jit(solution)/shard_map/ppermute | solution.py:53
  114.2 14.9 %collective-permute-start.14 = (f32[16,16384]{1,0:T(8,128)S(1)}, f32[16,16384]{1,0:T(8,128)S(1)}, u32[]{:S(2)}, u32[]{:S(2)}) collective-permute-start(f32[16,16384]{1,0:T(8,128)S(1)} %slice.65), channel_id=1, source_target_pairs={{0,64},{4,12},{8,72},{12,4},{16,80},{20,28},{24,88},{28,20},{32,96... | collective-permute-start | bytes 3145736 | tf_op jit(solution)/shard_map/ppermute | solution.py:53
  129.2 21.4 %collective-permute-start.15 = (f32[8,16384]{1,0:T(8,128)S(1)}, f32[8,16384]{1,0:T(8,128)S(1)}, u32[]{:S(2)}, u32[]{:S(2)}) collective-permute-start(f32[8,16384]{1,0:T(8,128)S(1)} %slice.67), channel_id=1, source_target_pairs={{0,16},{4,132},{8,24},{12,140},{16,0},{20,148},{24,8},{28,156},{32... | collective-permute-start | bytes 1572872 | tf_op jit(solution)/shard_map/ppermute | solution.py:53
  150.8 8.2 %collective-permute-start.16 = (f32[4,16384]{1,0:T(4,128)S(1)}, f32[4,16384]{1,0:T(4,128)S(1)}, u32[]{:S(2)}, u32[]{:S(2)}) collective-permute-start(f32[4,16384]{1,0:T(4,128)S(1)} %slice.69), channel_id=1, source_target_pairs={{0,128},{4,20},{8,136},{12,28},{16,144},{20,4},{24,152},{28,12},{3... | collective-permute-start | bytes 786440 | tf_op jit(solution)/shard_map/ppermute | solution.py:53
  159.1 10.4 %collective-permute-start.17 = (f32[2,16384]{1,0:T(2,128)S(1)}, f32[2,16384]{1,0:T(2,128)S(1)}, u32[]{:S(2)}, u32[]{:S(2)}) collective-permute-start(f32[2,16384]{1,0:T(2,128)S(1)} %slice.71), channel_id=1, source_target_pairs={{0,32},{4,36},{8,40},{12,44},{16,48},{20,52},{24,56},{28,60},{32,0... | collective-permute-start | bytes 393224 | tf_op jit(solution)/shard_map/ppermute | solution.py:53
  170.3 5.2 %collective-permute-start.18 = (f32[16,128]{1,0:T(8,128)S(1)}, f32[16,128]{1,0:T(8,128)S(1)}, u32[]{:S(2)}, u32[]{:S(2)}) collective-permute-start(f32[16,128]{1,0:T(8,128)S(1)} %fusion.18), channel_id=1, source_target_pairs={{0,1},{1,0},{2,3},{3,2},{4,5},{5,4},{6,7},{7,6},{8,9},{9,8},{10,11... | collective-permute-start | bytes 24584 | tf_op jit(solution)/shard_map/ppermute | solution.py:21

commit v4 on v3

--- a/solution.py
+++ b/solution.py
@@ -30,28 +30,66 @@
     return {0: plain, 1: plain}
 
 
-def scatter_layout(size, per):
+def row_layout(size, per):
     steps = scatter_steps(size)
-    rounds = len(steps[0])
     table = np.zeros((size, size * per), np.int32)
     for d in range(size):
+        seq = steps[d & 1]
+        rest = seq[2:]
         for b in range(size):
-            seq = steps[b & 1]
             pos = 0
-            for r, st in enumerate(seq):
-                pos |= (((b ^ d) // st) % 2) << (rounds - 1 - r)
+            for r, st in enumerate(rest):
+                pos |= (((b ^ d) // st) % 2) << (len(rest) - 1 - r)
+            w = (b & 1) * 2 + (b // seq[1]) % 2
             for t in range(per):
-                table[d, pos * per + t] = b * per + t
+                table[d, (pos * 4 + w) * per + t] = b * per + t
     return table
 
 
-def halving_scatter(x, axis, size):
+def column_round(x, axis, size, r):
     steps = scatter_steps(size)
-    for r in range(len(steps[0])):
+    idx = lax.axis_index(axis)
+    st = jnp.asarray(np.array([steps[0][r], steps[1][r]], np.int32))[idx % 2]
+    bit = (idx // st) % 2
+    half = x.shape[1] // 2
+    keep = lax.dynamic_slice_in_dim(x, bit * half, half, 1)
+    send = lax.dynamic_slice_in_dim(x, (1 - bit) * half, half, 1)
+    return keep + lax.ppermute(send, axis, [(i, i ^ steps[i & 1][r]) for i in range(size)])
+
+
+def row_rounds(x, axis, size):
+    steps = scatter_steps(size)
+    for r in range(2, len(steps[0])):
         half = x.shape[0] // 2
         perm = [(i, i ^ steps[i & 1][r]) for i in range(size)]
         x = x[:half] + lax.ppermute(x[half:], axis, perm)
     return x
+
+
+def gather_own_rows(x, axis, size, per):
+    steps = scatter_steps(size)
+    idx = lax.axis_index(axis)
+    c = idx % 2
+    st2 = jnp.asarray(np.array([steps[0][1], steps[1][1]], np.int32))
+    own_st, other_st = st2[c], st2[1 - c]
+    j = (idx // own_st) % 2
+    j1 = (idx // other_st) % 2
+
+    def rows_of(b):
+        w = (b % 2) * 2 + (b // own_st) % 2
+        return lax.dynamic_slice_in_dim(x, w * per, per, 0)
+
+    same = lax.ppermute(rows_of(idx ^ own_st), axis, [(i, i ^ steps[i & 1][1]) for i in range(size)])
+    pair = lax.ppermute(rows_of(idx ^ 1), axis, [(i, i ^ 1) for i in range(size)])
+    cross = lax.ppermute(
+        rows_of(idx ^ 1 ^ own_st), axis, [(i, i ^ 1 ^ steps[i & 1][1]) for i in range(size)]
+    )
+    pieces = jnp.stack([rows_of(idx), same, pair, cross])
+    high = jnp.array([0, 0, 1, 1], jnp.int32)
+    low = jnp.array([0, 1, 0, 1], jnp.int32)
+    src = jnp.where(high == c, jnp.where(low == j, 0, 1), jnp.where(low == j1, 2, 3))
+    picked = jnp.take(pieces, src, axis=0)
+    return jnp.swapaxes(picked, 0, 1).reshape(per, -1)
 
 
 def body(field, g_first, g_second, g_third, g_fourth, h_second, h_third, h_fourth, *, n_space, n_pa, n_pb):
@@ -72,23 +110,21 @@
     gram = butterfly_sum(
         jnp.dot(sketch.T, sketch, precision=highest, preferred_element_type=jnp.float32), "space", n_space
     )
+    projected = lax.dot_general(
+        sketch, flat, (((0,), (0,)), ((), ())), precision=lax.Precision.HIGH, preferred_element_type=jnp.float32
+    )
+    projected = column_round(column_round(projected, "space", n_space, 0), "space", n_space, 1)
     lower = jnp.linalg.cholesky(gram)
-    basis = lax.linalg.triangular_solve(
-        lower, sketch, left_side=False, lower=True, transpose_a=True
+    inverse = lax.linalg.triangular_solve(
+        lower, jnp.eye(RANK, dtype=jnp.float32), left_side=True, lower=True
     )
+    basis = jnp.dot(sketch, inverse.T, precision=highest, preferred_element_type=jnp.float32)
     per = RANK // n_space
-    order = jnp.asarray(scatter_layout(n_space, per))[lax.axis_index("space")]
-    core_flat = halving_scatter(
-        lax.dot_general(
-            jnp.take(basis, order, axis=1),
-            flat,
-            (((0,), (0,)), ((), ())),
-            precision=lax.Precision.HIGH,
-            preferred_element_type=jnp.float32,
-        ),
-        "space",
-        n_space,
+    order = jnp.asarray(row_layout(n_space, per))[lax.axis_index("space")]
+    core_part = jnp.dot(
+        jnp.take(inverse, order, axis=0), projected, precision=lax.Precision.HIGH, preferred_element_type=jnp.float32
     )
+    core_flat = gather_own_rows(row_rounds(core_part, "space", n_space), "space", n_space, per)
     own_rank = core_flat.shape[0]
     psi = (
         h_second[:, None, None, :] * h_third[None, :, None, :] * h_fourth[None, None, :, :]

time: 176 us -> 194 us (1.10); the launches traced: 176 us -> 192 us
  waiting for transfers between devices: 99.4 us -> 87.5 us
  between operations: 0.89 us -> 10.3 us
  local copies, waits for them, and re-layouts: 2.98 us -> 11.7 us
  matrix products: 16.7 us -> 20.1 us
  other arithmetic: 27.4 us -> 30.8 us
  starting transfers between devices: 28.8 us -> 31.1 us
    ppermute x6 -> x9, waiting for transfers between devices: 78.3 us -> 47.1 us  [the longest x4 40.4 us: row_rounds(): x = x[:half] + lax.ppermute(x[half:], axis, perm)]
    ppermute x4, waiting for transfers between devices: 9.09 us -> 31.4 us  [butterfly_sum(): far = lax.ppermute(x, axis, [(i, i ^ 2 * step) for i in range(size)])]
    dynamic_slice x0 -> x3, local copies, waits for them, and re-layouts: none -> 4.55 us  [the longest x2 3.96 us: column_round(): send = lax.dynamic_slice_in_dim(x, (1 - bit) * half, half, 1)]
    unnamed x8 -> x16, local copies, waits for them, and re-layouts: 0.03 us -> 4.03 us
    dot_general x1 -> x3, matrix products: 6.34 us -> 9.78 us  [the longest x1 6.23 us: body(): lax.dot_general(sketch, flat, (((0,), (0,)), ((), ())), precision=lax.Pre...]
    add x6 -> x5, other arithmetic: 0.96 us -> 4.16 us  [the longest x1 3.9 us: column_round(): keep + lax.ppermute(send, axis, [(i, i ^ steps[i & 1][r]) for i in range(...]
    ppermute x6 -> x9, starting transfers between devices: 9.77 us -> 11.7 us  [the longest x4 7.61 us: row_rounds(): x = x[:half] + lax.ppermute(x[half:], axis, perm)]
    another operation x2 -> x3, other arithmetic: 10.5 us -> 10.5 us  [the longest x2 10.5 us: body(): lax.linalg.triangular_solve(lower, jnp.eye(RANK, dtype=jnp.float32), left...]
  transfers between devices with their start and end apart: 19 -> 22, of which waited for: 17 -> 17; matrix products, arithmetic and copies ran while one was open for 2% -> 15% of each run, Pallas kernels for 0% -> 0%
where the time goes in v4:
time: 194 us; the launch traced here: 192 us
  waiting for transfers between devices  87.5 us (45%)
  starting transfers between devices  31.1 us (16%)
  other arithmetic  30.8 us (16%)
  matrix products  20.1 us (10%)
  local copies, waits for them, and re-layouts  11.7 us (6%)
  between operations  10.3 us (5%)
    ppermute x4, waiting for transfers between devices, row_rounds(): x = x[:half] + lax.ppermute(x[half:], axis, perm)  40.4 us
    ppermute x4, waiting for transfers between devices, butterfly_sum(): far = lax.ppermute(x, axis, [(i, i ^ 2 * step) for i in range(size)])  31.4 us
    another operation x3, other arithmetic, body(): lower = jnp.linalg.cholesky(gram)  12.4 us
    another operation x2, other arithmetic, body(): lax.linalg.triangular_solve(lower, jnp.eye(RANK, dtype=jnp.float32), left...  10.5 us
    dot_general x1, matrix products, body(): jnp.dot(flat, omega, precision=lax.Precision.HIGH, preferred_element_type...  9.15 us
    ppermute x4, starting transfers between devices, butterfly_sum(): far = lax.ppermute(x, axis, [(i, i ^ 2 * step) for i in range(size)])  7.8 us
    ppermute x4, starting transfers between devices, row_rounds(): x = x[:half] + lax.ppermute(x[half:], axis, perm)  7.61 us
    ppermute x4, starting transfers between devices, butterfly_sum(): near = lax.ppermute(x, axis, [(i, i ^ step) for i in range(size)])  6.63 us
  transfers between devices with their start and end apart: 22, of which 17 were waited for; matrix products, arithmetic and copies ran while one was open for 15% of the time, Pallas kernels for 0%

profile of v4, /device:TPU:24, one launch (start us, length us, event | category | flops | bytes accessed | tf_op | source)
XLA Modules:
  0.0 191.5 jit_solution(2818228286732898861)
XLA Ops:
  2.1 9.1 %fusion.7 = f32[128,128]{0,1:T(8,128)S(1)} fusion(f32[128,8,16,8,16]{0,4,3,2,1:T(8,128)} %param.14, f32[16,128]{1,0:T(8,128)} %param.18, f32[8,16,8,128]{3,2,1,0:T(8,128)S(1)} %broadcast_multiply_fusion.1), kind=kOutput, calls=%fused_computation.10 | convolution fusion | flops 1612709888 | bytes 8986624 | tf_op jit(solution)/shard_map/dot_general | solution.py:108
  11.2 3.1 %collective-permute-start = (f32[128,128]{0,1:T(8,128)S(1)}, f32[128,128]{0,1:T(8,128)S(1)}, u32[]{:S(2)}, u32[]{:S(2)}) collective-permute-start(f32[128,128]{0,1:T(8,128)S(1)} %fusion.7), channel_id=1, source_target_pairs={{0,1},{1,0},{2,3},{3,2},{4,5},{5,4},{6,7},{7,6},{8,9},{9,8},{10,11... | collective-permute-start | bytes 196616 | tf_op jit(solution)/shard_map/ppermute | solution.py:15
  20.4 6.2 %fusion.23 = f32[128,16384]{1,0:T(8,128)S(1)} fusion(f32[128,128]{0,1:T(8,128)S(1)} %add_add_fusion.3, f32[128,16384]{0,1:T(8,128)} %bitcast.43), kind=kOutput, calls=%fused_computation.61 | convolution fusion | flops 1610612736 | bytes 16842752 | tf_op jit(solution)/shard_map/dot_general | solution.py:113
  26.7 2.5 %constant_dynamic-slice_fusion.4 = f32[128,8192]{1,0:T(8,128)} fusion(f32[128,16384]{1,0:T(8,128)S(1)} %fusion.23, s32[]{:T(128)S(6)} %select_n.177), kind=kLoop, calls=%fused_computation.48 | loop fusion | bytes 8388612 | tf_op jit(solution)/shard_map/dynamic_slice | solution.py:56
  29.1 2.0 %copy-done = f32[128,16384]{1,0:T(8,128)} copy-done((f32[128,16384]{1,0:T(8,128)}, f32[128,16384]{1,0:T(8,128)S(1)}, u32[]{:S(2)}) %copy-start) | copy-done | bytes 8388632
  33.8 4.9 %collective-permute-done.12 = f32[128,8192]{1,0:T(8,128)} collective-permute-done((f32[128,8192]{1,0:T(8,128)}, f32[128,8192]{1,0:T(8,128)}, u32[]{:S(2)}, u32[]{:S(2)}) %collective-permute-start.12) | collective-permute-done | bytes 4194336 | tf_op jit(solution)/shard_map/ppermute | solution.py:57
  38.7 3.9 %dynamic-slice_add_fusion = f32[128,8192]{1,0:T(8,128)S(1)} fusion(f32[128,8192]{1,0:T(8,128)} %collective-permute-done.12, f32[128,16384]{1,0:T(8,128)} %copy-done, s32[]{:T(128)S(6)} %select_n.176), kind=kLoop, calls=%fused_computation.4 | loop fusion | flops 1048576 | bytes 12582916 | tf_op jit(solution)/shard_map/add | solution.py:57
  50.9 23.5 %collective-permute-done.4 = f32[128,128]{0,1:T(8,128)S(1)} collective-permute-done((f32[128,128]{0,1:T(8,128)S(1)}, f32[128,128]{0,1:T(8,128)S(1)}, u32[]{:S(2)}, u32[]{:S(2)}) %collective-permute-start.4) | collective-permute-done | bytes 65568 | tf_op jit(solution)/shard_map/ppermute | solution.py:16
  74.5 3.4 %collective-permute-start.6 = (f32[128,128]{0,1:T(8,128)S(1)}, f32[128,128]{0,1:T(8,128)S(1)}, u32[]{:S(2)}, u32[]{:S(2)}) collective-permute-start(f32[128,128]{0,1:T(8,128)S(1)} %add_add_fusion.2), channel_id=1, source_target_pairs={{0,16},{4,20},{8,24},{12,28},{16,0},{20,4},{24,8},{28,12},{32,48},... | collective-permute-start | bytes 196616 | tf_op jit(solution)/shard_map/ppermute | solution.py:15
  77.9 5.3 %collective-permute-start.7 = (f32[128,128]{0,1:T(8,128)S(1)}, f32[128,128]{0,1:T(8,128)S(1)}, u32[]{:S(2)}, u32[]{:S(2)}) collective-permute-start(f32[128,128]{0,1:T(8,128)S(1)} %add_add_fusion.2), channel_id=1, source_target_pairs={{0,32},{4,36},{8,40},{12,44},{16,48},{20,52},{24,56},{28,60},{32,0... | collective-permute-start | bytes 196616 | tf_op jit(solution)/shard_map/ppermute | solution.py:16
  83.2 4.0 %collective-permute-done.7 = f32[128,128]{0,1:T(8,128)S(1)} collective-permute-done((f32[128,128]{0,1:T(8,128)S(1)}, f32[128,128]{0,1:T(8,128)S(1)}, u32[]{:S(2)}, u32[]{:S(2)}) %collective-permute-start.7) | collective-permute-done | bytes 65568 | tf_op jit(solution)/shard_map/ppermute | solution.py:16
  87.2 2.4 %collective-permute-done.8 = f32[128,128]{0,1:T(8,128)S(1)} collective-permute-done((f32[128,128]{0,1:T(8,128)S(1)}, f32[128,128]{0,1:T(8,128)S(1)}, u32[]{:S(2)}, u32[]{:S(2)}) %collective-permute-start.8) | collective-permute-done | bytes 65568 | tf_op jit(solution)/shard_map/ppermute | solution.py:17
  90.9 2.2 %collective-permute-start.11 = (f32[128,128]{0,1:T(8,128)S(1)}, f32[128,128]{0,1:T(8,128)S(1)}, u32[]{:S(2)}, u32[]{:S(2)}) collective-permute-start(f32[128,128]{0,1:T(8,128)S(1)} %add_add_fusion.1), channel_id=1, source_target_pairs={{0,192},{4,196},{8,200},{12,204},{16,208},{20,212},{24,216},{28,22... | collective-permute-start | bytes 196616 | tf_op jit(solution)/shard_map/ppermute | solution.py:17
  93.9 2.4 %collective-permute-done.10 = f32[128,128]{0,1:T(8,128)S(1)} collective-permute-done((f32[128,128]{0,1:T(8,128)S(1)}, f32[128,128]{0,1:T(8,128)S(1)}, u32[]{:S(2)}, u32[]{:S(2)}) %collective-permute-start.10) | collective-permute-done | bytes 65568 | tf_op jit(solution)/shard_map/ppermute | solution.py:16
  97.5 11.7 %cholesky.17 = f32[128,128]{1,0:T(8,128)S(1)} custom-call(f32[128,128]{1,0:T(8,128)S(1)} %fusion.13), custom_call_target="Cholesky" | custom-call | tf_op jit(solution)/shard_map/jit(cholesky)/cholesky | solution.py:117
  110.5 9.8 %custom-call.6 = f32[1,128,128]{1,2,0:T(8,128)S(1)} custom-call(f32[1,128,128]{2,1,0:T(8,128)S(1)} %fusion.10), custom_call_target="InvertDiagBlocksLowerTriangular" | custom-call | tf_op jit(solution)/shard_map/triangular_solve | solution.py:118
  121.3 2.6 %fusion.4 = f32[128,4096]{1,0:T(8,128)S(1)} fusion(f32[128,4096]{1,0:T(8,128)S(1)} %collective-permute-done.13, f32[128,8192]{1,0:T(8,128)} %copy-done.1, s32[]{:T(128)S(6)} %select_n.180, f32[128,128]{1,0:T(8,128)S(1)} %gather_fusion, pred[128]{0:T(512)(128)(4,1)S(1)} %compare_and_fusion), kind=kOutput, calls=%fused_computation.7 | convolution fusion | flops 403193856 | bytes 6357124 | tf_op jit(solution)/shard_map/dot_general | solution.py:124
  124.2 14.7 %collective-permute-done.14 = f32[64,4096]{1,0:T(8,128)S(1)} collective-permute-done((f32[64,4096]{1,0:T(8,128)S(1)}, f32[64,4096]{1,0:T(8,128)S(1)}, u32[]{:S(2)}, u32[]{:S(2)}) %collective-permute-start.14) | collective-permute-done | bytes 1048608 | tf_op jit(solution)/shard_map/ppermute | solution.py:65
  139.1 4.5 %collective-permute-start.15 = (f32[32,4096]{1,0:T(8,128)S(1)}, f32[32,4096]{1,0:T(8,128)S(1)}, u32[]{:S(2)}, u32[]{:S(2)}) collective-permute-start(f32[32,4096]{1,0:T(8,128)S(1)} %slice.49), channel_id=1, source_target_pairs={{0,16},{4,132},{8,24},{12,140},{16,0},{20,148},{24,8},{28,156},{32... | collective-permute-start | bytes 1572872 | tf_op jit(solution)/shard_map/ppermute | solution.py:65
  143.6 18.4 %collective-permute-done.15 = f32[32,4096]{1,0:T(8,128)S(1)} collective-permute-done((f32[32,4096]{1,0:T(8,128)S(1)}, f32[32,4096]{1,0:T(8,128)S(1)}, u32[]{:S(2)}, u32[]{:S(2)}) %collective-permute-start.15) | collective-permute-done | bytes 524320 | tf_op jit(solution)/shard_map/ppermute | solution.py:65
  170.4 2.6 %collective-permute-start.17 = (f32[8,4096]{1,0:T(8,128)S(1)}, f32[8,4096]{1,0:T(8,128)S(1)}, u32[]{:S(2)}, u32[]{:S(2)}) collective-permute-start(f32[8,4096]{1,0:T(8,128)S(1)} %slice.53), channel_id=1, source_target_pairs={{0,32},{4,36},{8,40},{12,44},{16,48},{20,52},{24,56},{28,60},{32,0... | collective-permute-start | bytes 393224 | tf_op jit(solution)/shard_map/ppermute | solution.py:65
  173.0 6.9 %collective-permute-done.17 = f32[8,4096]{1,0:T(8,128)S(1)} collective-permute-done((f32[8,4096]{1,0:T(8,128)S(1)}, f32[8,4096]{1,0:T(8,128)S(1)}, u32[]{:S(2)}, u32[]{:S(2)}) %collective-permute-start.17) | collective-permute-done | bytes 131104 | tf_op jit(solution)/shard_map/ppermute | solution.py:65
  180.2 2.0 %collective-permute-start.20 = (f32[2,4096]{1,0:T(2,128)S(1)}, f32[2,4096]{1,0:T(2,128)S(1)}, u32[]{:S(2)}, u32[]{:S(2)}) collective-permute-start(f32[2,4096]{1,0:T(2,128)S(1)} %get-tuple-element.6), channel_id=1, source_target_pairs={{0,12},{4,64},{8,4},{12,72},{16,28},{20,80},{24,20},{28,88},{32,44... | collective-permute-start | bytes 98312 | tf_op jit(solution)/shard_map/ppermute | solution.py:84
  188.8 2.1 %collective-permute-done.21 = f32[16,128]{1,0:T(8,128)S(1)} collective-permute-done((f32[16,128]{1,0:T(8,128)S(1)}, f32[16,128]{1,0:T(8,128)S(1)}, u32[]{:S(2)}, u32[]{:S(2)}) %collective-permute-start.21) | collective-permute-done | bytes 8224 | tf_op jit(solution)/shard_map/ppermute | solution.py:21
  (84 shorter events, 30.9 us)
Async XLA Ops:
  11.2 5.9 %collective-permute-start = (f32[128,128]{0,1:T(8,128)S(1)}, f32[128,128]{0,1:T(8,128)S(1)}, u32[]{:S(2)}, u32[]{:S(2)}) collective-permute-start(f32[128,128]{0,1:T(8,128)S(1)} %fusion.7), channel_id=1, source_target_pairs={{0,1},{1,0},{2,3},{3,2},{4,5},{5,4},{6,7},{7,6},{8,9},{9,8},{10,11... | collective-permute-start | bytes 196616 | tf_op jit(solution)/shard_map/ppermute | solution.py:15
  14.3 4.3 %collective-permute-start.1 = (f32[128,128]{0,1:T(8,128)S(1)}, f32[128,128]{0,1:T(8,128)S(1)}, u32[]{:S(2)}, u32[]{:S(2)}) collective-permute-start(f32[128,128]{0,1:T(8,128)S(1)} %fusion.7), channel_id=1, source_target_pairs={{0,2},{1,3},{2,0},{3,1},{4,6},{5,7},{6,4},{7,5},{8,10},{9,11},{10,... | collective-permute-start | bytes 196616 | tf_op jit(solution)/shard_map/ppermute | solution.py:16
  14.9 5.5 %collective-permute-start.2 = (f32[128,128]{0,1:T(8,128)S(1)}, f32[128,128]{0,1:T(8,128)S(1)}, u32[]{:S(2)}, u32[]{:S(2)}) collective-permute-start(f32[128,128]{0,1:T(8,128)S(1)} %fusion.7), channel_id=1, source_target_pairs={{0,3},{1,2},{2,1},{3,0},{4,7},{5,6},{6,5},{7,4},{8,11},{9,10},{10,... | collective-permute-start | bytes 196616 | tf_op jit(solution)/shard_map/ppermute | solution.py:17
  31.2 7.5 %collective-permute-start.12 = (f32[128,8192]{1,0:T(8,128)}, f32[128,8192]{1,0:T(8,128)}, u32[]{:S(2)}, u32[]{:S(2)}) collective-permute-start(f32[128,8192]{1,0:T(8,128)} %constant_dynamic-slice_fusion.4), channel_id=1, source_target_pairs={{0,4},{4,0},{8,12},{12,8},{16,20},{20,16},{24,28},{28,24},{32,36},... | collective-permute-start | bytes 12582920 | tf_op jit(solution)/shard_map/ppermute | solution.py:57
  46.0 75.2 %collective-permute-start.13 = (f32[128,4096]{1,0:T(8,128)}, f32[128,4096]{1,0:T(8,128)S(1)}, u32[]{:S(2)}, u32[]{:S(2)}) collective-permute-start(f32[128,4096]{1,0:T(8,128)} %constant_dynamic-slice_fusion.2), channel_id=1, source_target_pairs={{0,8},{4,68},{8,0},{12,76},{16,24},{20,84},{24,16},{28,92},{32,40}... | collective-permute-start | bytes 6291464 | tf_op jit(solution)/shard_map/ppermute | solution.py:57
  48.2 2.6 %collective-permute-start.3 = (f32[128,128]{0,1:T(8,128)S(1)}, f32[128,128]{0,1:T(8,128)S(1)}, u32[]{:S(2)}, u32[]{:S(2)}) collective-permute-start(f32[128,128]{0,1:T(8,128)S(1)} %fusion.21), channel_id=1, source_target_pairs={{0,4},{4,0},{8,12},{12,8},{16,20},{20,16},{24,28},{28,24},{32,36},... | collective-permute-start | bytes 196616 | tf_op jit(solution)/shard_map/ppermute | solution.py:15
  48.3 26.1 %collective-permute-start.4 = (f32[128,128]{0,1:T(8,128)S(1)}, f32[128,128]{0,1:T(8,128)S(1)}, u32[]{:S(2)}, u32[]{:S(2)}) collective-permute-start(f32[128,128]{0,1:T(8,128)S(1)} %fusion.21), channel_id=1, source_target_pairs={{0,8},{4,12},{8,0},{12,4},{16,24},{20,28},{24,16},{28,20},{32,40},... | collective-permute-start | bytes 196616 | tf_op jit(solution)/shard_map/ppermute | solution.py:16
  48.9 25.6 %collective-permute-start.5 = (f32[128,128]{0,1:T(8,128)S(1)}, f32[128,128]{0,1:T(8,128)S(1)}, u32[]{:S(2)}, u32[]{:S(2)}) collective-permute-start(f32[128,128]{0,1:T(8,128)S(1)} %fusion.21), channel_id=1, source_target_pairs={{0,12},{4,8},{8,4},{12,0},{16,28},{20,24},{24,20},{28,16},{32,44},... | collective-permute-start | bytes 196616 | tf_op jit(solution)/shard_map/ppermute | solution.py:17
  74.5 8.7 %collective-permute-start.6 = (f32[128,128]{0,1:T(8,128)S(1)}, f32[128,128]{0,1:T(8,128)S(1)}, u32[]{:S(2)}, u32[]{:S(2)}) collective-permute-start(f32[128,128]{0,1:T(8,128)S(1)} %add_add_fusion.2), channel_id=1, source_target_pairs={{0,16},{4,20},{8,24},{12,28},{16,0},{20,4},{24,8},{28,12},{32,48},... | collective-permute-start | bytes 196616 | tf_op jit(solution)/shard_map/ppermute | solution.py:15
  77.9 9.3 %collective-permute-start.7 = (f32[128,128]{0,1:T(8,128)S(1)}, f32[128,128]{0,1:T(8,128)S(1)}, u32[]{:S(2)}, u32[]{:S(2)}) collective-permute-start(f32[128,128]{0,1:T(8,128)S(1)} %add_add_fusion.2), channel_id=1, source_target_pairs={{0,32},{4,36},{8,40},{12,44},{16,48},{20,52},{24,56},{28,60},{32,0... | collective-permute-start | bytes 196616 | tf_op jit(solution)/shard_map/ppermute | solution.py:16
  83.2 6.4 %collective-permute-start.8 = (f32[128,128]{0,1:T(8,128)S(1)}, f32[128,128]{0,1:T(8,128)S(1)}, u32[]{:S(2)}, u32[]{:S(2)}) collective-permute-start(f32[128,128]{0,1:T(8,128)S(1)} %add_add_fusion.2), channel_id=1, source_target_pairs={{0,48},{4,52},{8,56},{12,60},{16,32},{20,36},{24,40},{28,44},{32,1... | collective-permute-start | bytes 196616 | tf_op jit(solution)/shard_map/ppermute | solution.py:17
  89.6 6.6 %collective-permute-start.10 = (f32[128,128]{0,1:T(8,128)S(1)}, f32[128,128]{0,1:T(8,128)S(1)}, u32[]{:S(2)}, u32[]{:S(2)}) collective-permute-start(f32[128,128]{0,1:T(8,128)S(1)} %add_add_fusion.1), channel_id=1, source_target_pairs={{0,128},{4,132},{8,136},{12,140},{16,144},{20,148},{24,152},{28,15... | collective-permute-start | bytes 196616 | tf_op jit(solution)/shard_map/ppermute | solution.py:16
  90.9 5.7 %collective-permute-start.11 = (f32[128,128]{0,1:T(8,128)S(1)}, f32[128,128]{0,1:T(8,128)S(1)}, u32[]{:S(2)}, u32[]{:S(2)}) collective-permute-start(f32[128,128]{0,1:T(8,128)S(1)} %add_add_fusion.1), channel_id=1, source_target_pairs={{0,192},{4,196},{8,200},{12,204},{16,208},{20,212},{24,216},{28,22... | collective-permute-start | bytes 196616 | tf_op jit(solution)/shard_map/ppermute | solution.py:17
  93.1 4.3 %collective-permute-start.9 = (f32[128,128]{0,1:T(8,128)S(1)}, f32[128,128]{0,1:T(8,128)S(1)}, u32[]{:S(2)}, u32[]{:S(2)}) collective-permute-start(f32[128,128]{0,1:T(8,128)S(1)} %add_add_fusion.1), channel_id=1, source_target_pairs={{0,64},{4,68},{8,72},{12,76},{16,80},{20,84},{24,88},{28,92},{32,9... | collective-permute-start | bytes 196616 | tf_op jit(solution)/shard_map/ppermute | solution.py:15
  124.0 49.0 %copy-start.6 = (s32[4]{0:T(128)S(1)}, s32[4]{0:T(128)}, u32[]{:S(2)}) copy-start(s32[4]{0:T(128)} %constant.190.clone) | copy-start | bytes 52
  124.0 49.0 %copy-start.7 = (s32[4]{0:T(128)S(1)}, s32[4]{0:T(128)}, u32[]{:S(2)}) copy-start(s32[4]{0:T(128)} %constant.191.clone) | copy-start | bytes 52
  124.0 14.9 %collective-permute-start.14 = (f32[64,4096]{1,0:T(8,128)S(1)}, f32[64,4096]{1,0:T(8,128)S(1)}, u32[]{:S(2)}, u32[]{:S(2)}) collective-permute-start(f32[64,4096]{1,0:T(8,128)S(1)} %slice.47), channel_id=1, source_target_pairs={{0,64},{4,12},{8,72},{12,4},{16,80},{20,28},{24,88},{28,20},{32,96... | collective-permute-start | bytes 3145736 | tf_op jit(solution)/shard_map/ppermute | solution.py:65
  139.1 22.9 %collective-permute-start.15 = (f32[32,4096]{1,0:T(8,128)S(1)}, f32[32,4096]{1,0:T(8,128)S(1)}, u32[]{:S(2)}, u32[]{:S(2)}) collective-permute-start(f32[32,4096]{1,0:T(8,128)S(1)} %slice.49), channel_id=1, source_target_pairs={{0,16},{4,132},{8,24},{12,140},{16,0},{20,148},{24,8},{28,156},{32... | collective-permute-start | bytes 1572872 | tf_op jit(solution)/shard_map/ppermute | solution.py:65
  162.1 8.2 %collective-permute-start.16 = (f32[16,4096]{1,0:T(8,128)S(1)}, f32[16,4096]{1,0:T(8,128)S(1)}, u32[]{:S(2)}, u32[]{:S(2)}) collective-permute-start(f32[16,4096]{1,0:T(8,128)S(1)} %slice.51), channel_id=1, source_target_pairs={{0,128},{4,20},{8,136},{12,28},{16,144},{20,4},{24,152},{28,12},{3... | collective-permute-start | bytes 786440 | tf_op jit(solution)/shard_map/ppermute | solution.py:65
  170.4 9.6 %collective-permute-start.17 = (f32[8,4096]{1,0:T(8,128)S(1)}, f32[8,4096]{1,0:T(8,128)S(1)}, u32[]{:S(2)}, u32[]{:S(2)}) collective-permute-start(f32[8,4096]{1,0:T(8,128)S(1)} %slice.53), channel_id=1, source_target_pairs={{0,32},{4,36},{8,40},{12,44},{16,48},{20,52},{24,56},{28,60},{32,0... | collective-permute-start | bytes 393224 | tf_op jit(solution)/shard_map/ppermute | solution.py:65
  180.0 4.0 %collective-permute-start.18 = (f32[2,4096]{1,0:T(2,128)S(1)}, f32[2,4096]{1,0:T(2,128)S(1)}, u32[]{:S(2)}, u32[]{:S(2)}) collective-permute-start(f32[2,4096]{1,0:T(2,128)S(1)} %get-tuple-element.8), channel_id=1, source_target_pairs={{0,8},{4,68},{8,0},{12,76},{16,24},{20,84},{24,16},{28,92},{32,40}... | collective-permute-start | bytes 98312 | tf_op jit(solution)/shard_map/ppermute | solution.py:82
  180.1 3.9 %collective-permute-start.19 = (f32[2,4096]{1,0:T(2,128)S(1)}, f32[2,4096]{1,0:T(2,128)S(1)}, u32[]{:S(2)}, u32[]{:S(2)}) collective-permute-start(f32[2,4096]{1,0:T(2,128)S(1)} %get-tuple-element.7), channel_id=1, source_target_pairs={{0,4},{4,0},{8,12},{12,8},{16,20},{20,16},{24,28},{28,24},{32,36},... | collective-permute-start | bytes 98312 | tf_op jit(solution)/shard_map/ppermute | solution.py:83
  180.2 3.8 %collective-permute-start.20 = (f32[2,4096]{1,0:T(2,128)S(1)}, f32[2,4096]{1,0:T(2,128)S(1)}, u32[]{:S(2)}, u32[]{:S(2)}) collective-permute-start(f32[2,4096]{1,0:T(2,128)S(1)} %get-tuple-element.6), channel_id=1, source_target_pairs={{0,12},{4,64},{8,4},{12,72},{16,28},{20,80},{24,20},{28,88},{32,44... | collective-permute-start | bytes 98312 | tf_op jit(solution)/shard_map/ppermute | solution.py:84
  185.7 5.2 %collective-permute-start.21 = (f32[16,128]{1,0:T(8,128)S(1)}, f32[16,128]{1,0:T(8,128)S(1)}, u32[]{:S(2)}, u32[]{:S(2)}) collective-permute-start(f32[16,128]{1,0:T(8,128)S(1)} %fusion.24), channel_id=1, source_target_pairs={{0,1},{1,0},{2,3},{3,2},{4,5},{5,4},{6,7},{7,6},{8,9},{9,8},{10,11... | collective-permute-start | bytes 24584 | tf_op jit(solution)/shard_map/ppermute | solution.py:21
  (6 other events, 134.0 us)

commit v5 on v4

--- a/solution.py
+++ b/solution.py
@@ -8,9 +8,9 @@
 RANK = 128
 
 
-def butterfly_sum(x, axis, size):
-    step = 1
-    while step < size:
+def butterfly_sum(x, axis, size, step=1, stop=None):
+    stop = size if stop is None else stop
+    while step < stop:
         if step * 4 <= size:
             near = lax.ppermute(x, axis, [(i, i ^ step) for i in range(size)])
             far = lax.ppermute(x, axis, [(i, i ^ (2 * step)) for i in range(size)])
@@ -107,13 +107,16 @@
     ).reshape(width, RANK)
     partial_sketch = jnp.dot(flat, omega, precision=lax.Precision.HIGH, preferred_element_type=jnp.float32)
     sketch = butterfly_sum(partial_sketch, ("pa", "pb"), n_pa * n_pb)
-    gram = butterfly_sum(
-        jnp.dot(sketch.T, sketch, precision=highest, preferred_element_type=jnp.float32), "space", n_space
+    gram_part = jnp.dot(sketch.T, sketch, precision=highest, preferred_element_type=jnp.float32)
+    gram_part = butterfly_sum(gram_part, "space", n_space, 1, 4)
+    sketch_late, gram_part = lax.optimization_barrier((sketch, gram_part))
+    gram = butterfly_sum(gram_part, "space", n_space, 4)
+    projected = lax.dot_general(
+        sketch_late, flat, (((0,), (0,)), ((), ())), precision=lax.Precision.HIGH, preferred_element_type=jnp.float32
     )
-    projected = lax.dot_general(
-        sketch, flat, (((0,), (0,)), ((), ())), precision=lax.Precision.HIGH, preferred_element_type=jnp.float32
-    )
-    projected = column_round(column_round(projected, "space", n_space, 0), "space", n_space, 1)
+    projected = column_round(projected, "space", n_space, 0)
+    projected, gram = lax.optimization_barrier((projected, gram))
+    projected = column_round(projected, "space", n_space, 1)
     lower = jnp.linalg.cholesky(gram)
     inverse = lax.linalg.triangular_solve(
         lower, jnp.eye(RANK, dtype=jnp.float32), left_side=True, lower=True

time: 194 us -> 167 us (0.86)
  waiting for transfers between devices: 87.5 us -> 62 us
    ppermute x4, waiting for transfers between devices: 31.4 us -> 3.44 us  [butterfly_sum(): far = lax.ppermute(x, axis, [(i, i ^ 2 * step) for i in range(size)])]
    ppermute x2, waiting for transfers between devices: 4.91 us -> 0.01 us  [column_round(): lax.ppermute(send, axis, [(i, i ^ steps[i & 1][r]) for i in range(size)])]
    ppermute x4, starting transfers between devices: 7.8 us -> 12.1 us  [butterfly_sum(): far = lax.ppermute(x, axis, [(i, i ^ 2 * step) for i in range(size)])]
    ppermute x4, starting transfers between devices: 6.63 us -> 2.4 us  [butterfly_sum(): near = lax.ppermute(x, axis, [(i, i ^ step) for i in range(size)])]
    ppermute x4, waiting for transfers between devices: 4.69 us -> 8.6 us  [butterfly_sum(): farther = lax.ppermute(x, axis, [(i, i ^ 3 * step) for i in range(size)])]
    ppermute x1, waiting for transfers between devices: 0.01 us -> 2.02 us  [gather_own_rows(): lax.ppermute(rows_of(idx ^ 1 ^ own_st), axis, [(i, i ^ 1 ^ steps[i & 1][1...]
    ppermute x1, starting transfers between devices: 2.03 us -> 0.08 us  [gather_own_rows(): lax.ppermute(rows_of(idx ^ 1 ^ own_st), axis, [(i, i ^ 1 ^ steps[i & 1][1...]
  transfers between devices with their start and end apart: 22 -> 22, of which waited for: 17 -> 15; matrix products, arithmetic and copies ran while one was open for 15% -> 17% of each run, Pallas kernels for 0% -> 0%
where the time goes in v5:
time: 167 us; the launch traced here: 165 us
  waiting for transfers between devices  62 us (37%)
  other arithmetic  30.9 us (19%)
  starting transfers between devices  30.3 us (18%)
  matrix products  20.1 us (12%)
  local copies, waits for them, and re-layouts  11.7 us (7%)
  between operations  10.3 us (6%)
    ppermute x4, waiting for transfers between devices, row_rounds(): x = x[:half] + lax.ppermute(x[half:], axis, perm)  39.7 us
    another operation x3, other arithmetic, body(): lower = jnp.linalg.cholesky(gram)  12.4 us
    ppermute x4, starting transfers between devices, butterfly_sum(): far = lax.ppermute(x, axis, [(i, i ^ 2 * step) for i in range(size)])  12.1 us
    another operation x2, other arithmetic, body(): lax.linalg.triangular_solve(lower, jnp.eye(RANK, dtype=jnp.float32), left...  10.5 us
    dot_general x1, matrix products, body(): jnp.dot(flat, omega, precision=lax.Precision.HIGH, preferred_element_type...  9.15 us
    ppermute x4, waiting for transfers between devices, butterfly_sum(): farther = lax.ppermute(x, axis, [(i, i ^ 3 * step) for i in range(size)])  8.6 us
    ppermute x4, starting transfers between devices, row_rounds(): x = x[:half] + lax.ppermute(x[half:], axis, perm)  8.1 us
    dot_general x1, matrix products, body(): lax.dot_general(sketch_late, flat, (((0,), (0,)), ((), ())), precision=la...  6.23 us
  transfers between devices with their start and end apart: 22, of which 15 were waited for; matrix products, arithmetic and copies ran while one was open for 17% of the time, Pallas kernels for 0%

profile of v5, /device:TPU:24, one launch (start us, length us, event | category | flops | bytes accessed | tf_op | source)
XLA Modules:
  0.0 165.2 jit_solution(309646720685184405)
XLA Ops:
  2.1 9.1 %fusion.7 = f32[128,128]{0,1:T(8,128)S(1)} fusion(f32[128,8,16,8,16]{0,4,3,2,1:T(8,128)} %param.14, f32[16,128]{1,0:T(8,128)} %param.18, f32[8,16,8,128]{3,2,1,0:T(8,128)S(1)} %broadcast_multiply_fusion.1), kind=kOutput, calls=%fused_computation.10 | convolution fusion | flops 1612709888 | bytes 8986624 | tf_op jit(solution)/shard_map/dot_general | solution.py:108
  12.8 2.1 %collective-permute-start.2 = (f32[128,128]{0,1:T(8,128)S(1)}, f32[128,128]{0,1:T(8,128)S(1)}, u32[]{:S(2)}, u32[]{:S(2)}) collective-permute-start(f32[128,128]{0,1:T(8,128)S(1)} %fusion.7), channel_id=1, source_target_pairs={{0,3},{1,2},{2,1},{3,0},{4,7},{5,6},{6,5},{7,4},{8,11},{9,10},{10,... | collective-permute-start | bytes 196616 | tf_op jit(solution)/shard_map/ppermute | solution.py:17
  15.6 2.7 %collective-permute-done.2 = f32[128,128]{0,1:T(8,128)S(1)} collective-permute-done((f32[128,128]{0,1:T(8,128)S(1)}, f32[128,128]{0,1:T(8,128)S(1)}, u32[]{:S(2)}, u32[]{:S(2)}) %collective-permute-start.2) | collective-permute-done | bytes 65568 | tf_op jit(solution)/shard_map/ppermute | solution.py:17
  18.3 2.4 %collective-permute-done = f32[128,128]{0,1:T(8,128)S(1)} collective-permute-done((f32[128,128]{0,1:T(8,128)S(1)}, f32[128,128]{0,1:T(8,128)S(1)}, u32[]{:S(2)}, u32[]{:S(2)}) %collective-permute-start) | collective-permute-done | bytes 65568 | tf_op jit(solution)/shard_map/ppermute | solution.py:15
  21.0 2.0 %collective-permute-start.4 = (f32[128,128]{0,1:T(8,128)S(1)}, f32[128,128]{0,1:T(8,128)S(1)}, u32[]{:S(2)}, u32[]{:S(2)}) collective-permute-start(f32[128,128]{0,1:T(8,128)S(1)} %fusion.21), channel_id=1, source_target_pairs={{0,8},{4,12},{8,0},{12,4},{16,24},{20,28},{24,16},{28,20},{32,40},... | collective-permute-start | bytes 196616 | tf_op jit(solution)/shard_map/ppermute | solution.py:16
  23.2 2.1 %collective-permute-done.4 = f32[128,128]{0,1:T(8,128)S(1)} collective-permute-done((f32[128,128]{0,1:T(8,128)S(1)}, f32[128,128]{0,1:T(8,128)S(1)}, u32[]{:S(2)}, u32[]{:S(2)}) %collective-permute-start.4) | collective-permute-done | bytes 65568 | tf_op jit(solution)/shard_map/ppermute | solution.py:16
  26.7 6.2 %fusion.22 = f32[128,16384]{1,0:T(8,128)S(1)} fusion(f32[128,128]{0,1:T(8,128)S(1)} %add_add_fusion.3, f32[128,16384]{0,1:T(8,128)} %bitcast.43), kind=kOutput, calls=%fused_computation.60 | convolution fusion | flops 1610612736 | bytes 16842752 | tf_op jit(solution)/shard_map/dot_general | solution.py:114
  33.0 2.5 %constant_dynamic-slice_fusion.5 = f32[128,8192]{1,0:T(8,128)} fusion(f32[128,16384]{1,0:T(8,128)S(1)} %fusion.22, s32[]{:T(128)S(6)} %select_n.164), kind=kLoop, calls=%fused_computation.49 | loop fusion | bytes 8388612 | tf_op jit(solution)/shard_map/dynamic_slice | solution.py:56
  35.4 2.0 %copy-done = f32[128,16384]{1,0:T(8,128)} copy-done((f32[128,16384]{1,0:T(8,128)}, f32[128,16384]{1,0:T(8,128)S(1)}, u32[]{:S(2)}) %copy-start) | copy-done | bytes 8388632
  37.5 7.0 %collective-permute-start.8 = (f32[128,128]{0,1:T(8,128)S(1)}, f32[128,128]{0,1:T(8,128)S(1)}, u32[]{:S(2)}, u32[]{:S(2)}) collective-permute-start(f32[128,128]{0,1:T(8,128)S(1)} %add_add_fusion.2), channel_id=1, source_target_pairs={{0,32},{4,36},{8,40},{12,44},{16,48},{20,52},{24,56},{28,60},{32,0... | collective-permute-start | bytes 196616 | tf_op jit(solution)/shard_map/ppermute | solution.py:16
  47.3 3.6 %collective-permute-done.9 = f32[128,128]{0,1:T(8,128)S(1)} collective-permute-done((f32[128,128]{0,1:T(8,128)S(1)}, f32[128,128]{0,1:T(8,128)S(1)}, u32[]{:S(2)}, u32[]{:S(2)}) %collective-permute-start.9) | collective-permute-done | bytes 65568 | tf_op jit(solution)/shard_map/ppermute | solution.py:17
  53.4 2.2 %collective-permute-start.12 = (f32[128,128]{0,1:T(8,128)S(1)}, f32[128,128]{0,1:T(8,128)S(1)}, u32[]{:S(2)}, u32[]{:S(2)}) collective-permute-start(f32[128,128]{0,1:T(8,128)S(1)} %add_add_fusion.1), channel_id=1, source_target_pairs={{0,192},{4,196},{8,200},{12,204},{16,208},{20,212},{24,216},{28,22... | collective-permute-start | bytes 196616 | tf_op jit(solution)/shard_map/ppermute | solution.py:17
  59.9 3.9 %dynamic-slice_add_fusion = f32[128,8192]{1,0:T(8,128)S(1)} fusion(f32[128,8192]{1,0:T(8,128)} %collective-permute-done.6, f32[128,16384]{1,0:T(8,128)} %copy-done, s32[]{:T(128)S(6)} %select_n.163), kind=kLoop, calls=%fused_computation.4 | loop fusion | flops 1048576 | bytes 12582916 | tf_op jit(solution)/shard_map/add | solution.py:57
  63.8 1.9 %copy-done.1 = f32[128,8192]{1,0:T(8,128)} copy-done((f32[128,8192]{1,0:T(8,128)}, f32[128,8192]{1,0:T(8,128)S(1)}, u32[]{:S(2)}) %copy-start.1) | copy-done | bytes 4194328
  70.1 11.7 %cholesky.17 = f32[128,128]{1,0:T(8,128)S(1)} custom-call(f32[128,128]{1,0:T(8,128)S(1)} %fusion.13), custom_call_target="Cholesky" | custom-call | tf_op jit(solution)/shard_map/jit(cholesky)/cholesky | solution.py:120
  83.1 9.8 %custom-call.6 = f32[1,128,128]{1,2,0:T(8,128)S(1)} custom-call(f32[1,128,128]{2,1,0:T(8,128)S(1)} %fusion.10), custom_call_target="InvertDiagBlocksLowerTriangular" | custom-call | tf_op jit(solution)/shard_map/triangular_solve | solution.py:121
  93.8 2.6 %fusion.4 = f32[128,4096]{1,0:T(8,128)S(1)} fusion(f32[128,4096]{1,0:T(8,128)S(1)} %collective-permute-done.13, f32[128,8192]{1,0:T(8,128)} %copy-done.1, s32[]{:T(128)S(6)} %select_n.180, f32[128,128]{1,0:T(8,128)S(1)} %gather_fusion, pred[128]{0:T(512)(128)(4,1)S(1)} %compare_and_fusion), kind=kOutput, calls=%fused_computation.7 | convolution fusion | flops 403193856 | bytes 6357124 | tf_op jit(solution)/shard_map/dot_general | solution.py:127
  97.1 14.4 %collective-permute-done.14 = f32[64,4096]{1,0:T(8,128)S(1)} collective-permute-done((f32[64,4096]{1,0:T(8,128)S(1)}, f32[64,4096]{1,0:T(8,128)S(1)}, u32[]{:S(2)}, u32[]{:S(2)}) %collective-permute-start.14) | collective-permute-done | bytes 1048608 | tf_op jit(solution)/shard_map/ppermute | solution.py:65
  111.7 2.3 %collective-permute-start.15 = (f32[32,4096]{1,0:T(8,128)S(1)}, f32[32,4096]{1,0:T(8,128)S(1)}, u32[]{:S(2)}, u32[]{:S(2)}) collective-permute-start(f32[32,4096]{1,0:T(8,128)S(1)} %slice.49), channel_id=1, source_target_pairs={{0,16},{4,132},{8,24},{12,140},{16,0},{20,148},{24,8},{28,156},{32... | collective-permute-start | bytes 1572872 | tf_op jit(solution)/shard_map/ppermute | solution.py:65
  114.1 19.1 %collective-permute-done.15 = f32[32,4096]{1,0:T(8,128)S(1)} collective-permute-done((f32[32,4096]{1,0:T(8,128)S(1)}, f32[32,4096]{1,0:T(8,128)S(1)}, u32[]{:S(2)}, u32[]{:S(2)}) %collective-permute-start.15) | collective-permute-done | bytes 524320 | tf_op jit(solution)/shard_map/ppermute | solution.py:65
  141.9 4.1 %collective-permute-start.17 = (f32[8,4096]{1,0:T(8,128)S(1)}, f32[8,4096]{1,0:T(8,128)S(1)}, u32[]{:S(2)}, u32[]{:S(2)}) collective-permute-start(f32[8,4096]{1,0:T(8,128)S(1)} %slice.53), channel_id=1, source_target_pairs={{0,32},{4,36},{8,40},{12,44},{16,48},{20,52},{24,56},{28,60},{32,0... | collective-permute-start | bytes 393224 | tf_op jit(solution)/shard_map/ppermute | solution.py:65
  146.1 6.2 %collective-permute-done.17 = f32[8,4096]{1,0:T(8,128)S(1)} collective-permute-done((f32[8,4096]{1,0:T(8,128)S(1)}, f32[8,4096]{1,0:T(8,128)S(1)}, u32[]{:S(2)}, u32[]{:S(2)}) %collective-permute-start.17) | collective-permute-done | bytes 131104 | tf_op jit(solution)/shard_map/ppermute | solution.py:65
  153.8 2.0 %collective-permute-done.20 = f32[2,4096]{1,0:T(2,128)S(1)} collective-permute-done((f32[2,4096]{1,0:T(2,128)S(1)}, f32[2,4096]{1,0:T(2,128)S(1)}, u32[]{:S(2)}, u32[]{:S(2)}) %collective-permute-start.20) | collective-permute-done | bytes 32800 | tf_op jit(solution)/shard_map/ppermute | solution.py:84
  162.4 2.2 %collective-permute-done.21 = f32[16,128]{1,0:T(8,128)S(1)} collective-permute-done((f32[16,128]{1,0:T(8,128)S(1)}, f32[16,128]{1,0:T(8,128)S(1)}, u32[]{:S(2)}, u32[]{:S(2)}) %collective-permute-start.21) | collective-permute-done | bytes 8224 | tf_op jit(solution)/shard_map/ppermute | solution.py:21
  (84 shorter events, 30.4 us)
Async XLA Ops:
  11.2 4.4 %collective-permute-start.1 = (f32[128,128]{0,1:T(8,128)S(1)}, f32[128,128]{0,1:T(8,128)S(1)}, u32[]{:S(2)}, u32[]{:S(2)}) collective-permute-start(f32[128,128]{0,1:T(8,128)S(1)} %fusion.7), channel_id=1, source_target_pairs={{0,2},{1,3},{2,0},{3,1},{4,6},{5,7},{6,4},{7,5},{8,10},{9,11},{10,... | collective-permute-start | bytes 196616 | tf_op jit(solution)/shard_map/ppermute | solution.py:16
  12.8 5.5 %collective-permute-start.2 = (f32[128,128]{0,1:T(8,128)S(1)}, f32[128,128]{0,1:T(8,128)S(1)}, u32[]{:S(2)}, u32[]{:S(2)}) collective-permute-start(f32[128,128]{0,1:T(8,128)S(1)} %fusion.7), channel_id=1, source_target_pairs={{0,3},{1,2},{2,1},{3,0},{4,7},{5,6},{6,5},{7,4},{8,11},{9,10},{10,... | collective-permute-start | bytes 196616 | tf_op jit(solution)/shard_map/ppermute | solution.py:17
  14.9 5.8 %collective-permute-start = (f32[128,128]{0,1:T(8,128)S(1)}, f32[128,128]{0,1:T(8,128)S(1)}, u32[]{:S(2)}, u32[]{:S(2)}) collective-permute-start(f32[128,128]{0,1:T(8,128)S(1)} %fusion.7), channel_id=1, source_target_pairs={{0,1},{1,0},{2,3},{3,2},{4,5},{5,4},{6,7},{7,6},{8,9},{9,8},{10,11... | collective-permute-start | bytes 196616 | tf_op jit(solution)/shard_map/ppermute | solution.py:15
  21.0 4.4 %collective-permute-start.4 = (f32[128,128]{0,1:T(8,128)S(1)}, f32[128,128]{0,1:T(8,128)S(1)}, u32[]{:S(2)}, u32[]{:S(2)}) collective-permute-start(f32[128,128]{0,1:T(8,128)S(1)} %fusion.21), channel_id=1, source_target_pairs={{0,8},{4,12},{8,0},{12,4},{16,24},{20,28},{24,16},{28,20},{32,40},... | collective-permute-start | bytes 196616 | tf_op jit(solution)/shard_map/ppermute | solution.py:16
  23.0 3.8 %collective-permute-start.5 = (f32[128,128]{0,1:T(8,128)S(1)}, f32[128,128]{0,1:T(8,128)S(1)}, u32[]{:S(2)}, u32[]{:S(2)}) collective-permute-start(f32[128,128]{0,1:T(8,128)S(1)} %fusion.21), channel_id=1, source_target_pairs={{0,12},{4,8},{8,4},{12,0},{16,28},{20,24},{24,20},{28,16},{32,44},... | collective-permute-start | bytes 196616 | tf_op jit(solution)/shard_map/ppermute | solution.py:17
  23.0 3.8 %collective-permute-start.3 = (f32[128,128]{0,1:T(8,128)S(1)}, f32[128,128]{0,1:T(8,128)S(1)}, u32[]{:S(2)}, u32[]{:S(2)}) collective-permute-start(f32[128,128]{0,1:T(8,128)S(1)} %fusion.21), channel_id=1, source_target_pairs={{0,4},{4,0},{8,12},{12,8},{16,20},{20,16},{24,28},{28,24},{32,36},... | collective-permute-start | bytes 196616 | tf_op jit(solution)/shard_map/ppermute | solution.py:15
  37.5 22.4 %collective-permute-start.6 = (f32[128,8192]{1,0:T(8,128)}, f32[128,8192]{1,0:T(8,128)}, u32[]{:S(2)}, u32[]{:S(2)}) collective-permute-start(f32[128,8192]{1,0:T(8,128)} %constant_dynamic-slice_fusion.5), channel_id=1, source_target_pairs={{0,4},{4,0},{8,12},{12,8},{16,20},{20,16},{24,28},{28,24},{32,36},... | collective-permute-start | bytes 12582920 | tf_op jit(solution)/shard_map/ppermute | solution.py:57
  37.5 9.8 %collective-permute-start.8 = (f32[128,128]{0,1:T(8,128)S(1)}, f32[128,128]{0,1:T(8,128)S(1)}, u32[]{:S(2)}, u32[]{:S(2)}) collective-permute-start(f32[128,128]{0,1:T(8,128)S(1)} %add_add_fusion.2), channel_id=1, source_target_pairs={{0,32},{4,36},{8,40},{12,44},{16,48},{20,52},{24,56},{28,60},{32,0... | collective-permute-start | bytes 196616 | tf_op jit(solution)/shard_map/ppermute | solution.py:16
  44.5 6.4 %collective-permute-start.9 = (f32[128,128]{0,1:T(8,128)S(1)}, f32[128,128]{0,1:T(8,128)S(1)}, u32[]{:S(2)}, u32[]{:S(2)}) collective-permute-start(f32[128,128]{0,1:T(8,128)S(1)} %add_add_fusion.2), channel_id=1, source_target_pairs={{0,48},{4,52},{8,56},{12,60},{16,32},{20,36},{24,40},{28,44},{32,1... | collective-permute-start | bytes 196616 | tf_op jit(solution)/shard_map/ppermute | solution.py:17
  44.5 7.3 %collective-permute-start.7 = (f32[128,128]{0,1:T(8,128)S(1)}, f32[128,128]{0,1:T(8,128)S(1)}, u32[]{:S(2)}, u32[]{:S(2)}) collective-permute-start(f32[128,128]{0,1:T(8,128)S(1)} %add_add_fusion.2), channel_id=1, source_target_pairs={{0,16},{4,20},{8,24},{12,28},{16,0},{20,4},{24,8},{28,12},{32,48},... | collective-permute-start | bytes 196616 | tf_op jit(solution)/shard_map/ppermute | solution.py:15
  51.9 6.3 %collective-permute-start.11 = (f32[128,128]{0,1:T(8,128)S(1)}, f32[128,128]{0,1:T(8,128)S(1)}, u32[]{:S(2)}, u32[]{:S(2)}) collective-permute-start(f32[128,128]{0,1:T(8,128)S(1)} %add_add_fusion.1), channel_id=1, source_target_pairs={{0,128},{4,132},{8,136},{12,140},{16,144},{20,148},{24,152},{28,15... | collective-permute-start | bytes 196616 | tf_op jit(solution)/shard_map/ppermute | solution.py:16
  53.4 5.7 %collective-permute-start.12 = (f32[128,128]{0,1:T(8,128)S(1)}, f32[128,128]{0,1:T(8,128)S(1)}, u32[]{:S(2)}, u32[]{:S(2)}) collective-permute-start(f32[128,128]{0,1:T(8,128)S(1)} %add_add_fusion.1), channel_id=1, source_target_pairs={{0,192},{4,196},{8,200},{12,204},{16,208},{20,212},{24,216},{28,22... | collective-permute-start | bytes 196616 | tf_op jit(solution)/shard_map/ppermute | solution.py:17
  55.6 4.3 %collective-permute-start.10 = (f32[128,128]{0,1:T(8,128)S(1)}, f32[128,128]{0,1:T(8,128)S(1)}, u32[]{:S(2)}, u32[]{:S(2)}) collective-permute-start(f32[128,128]{0,1:T(8,128)S(1)} %add_add_fusion.1), channel_id=1, source_target_pairs={{0,64},{4,68},{8,72},{12,76},{16,80},{20,84},{24,88},{28,92},{32,9... | collective-permute-start | bytes 196616 | tf_op jit(solution)/shard_map/ppermute | solution.py:15
  67.2 26.6 %collective-permute-start.13 = (f32[128,4096]{1,0:T(8,128)}, f32[128,4096]{1,0:T(8,128)S(1)}, u32[]{:S(2)}, u32[]{:S(2)}) collective-permute-start(f32[128,4096]{1,0:T(8,128)} %constant_dynamic-slice_fusion.2), channel_id=1, source_target_pairs={{0,8},{4,68},{8,0},{12,76},{16,24},{20,84},{24,16},{28,92},{32,40}... | collective-permute-start | bytes 6291464 | tf_op jit(solution)/shard_map/ppermute | solution.py:57
  96.6 49.5 %copy-start.6 = (s32[4]{0:T(128)S(1)}, s32[4]{0:T(128)}, u32[]{:S(2)}) copy-start(s32[4]{0:T(128)} %constant.191.clone) | copy-start | bytes 52
  96.6 49.5 %copy-start.7 = (s32[4]{0:T(128)S(1)}, s32[4]{0:T(128)}, u32[]{:S(2)}) copy-start(s32[4]{0:T(128)} %constant.190.clone) | copy-start | bytes 52
  96.6 14.9 %collective-permute-start.14 = (f32[64,4096]{1,0:T(8,128)S(1)}, f32[64,4096]{1,0:T(8,128)S(1)}, u32[]{:S(2)}, u32[]{:S(2)}) collective-permute-start(f32[64,4096]{1,0:T(8,128)S(1)} %slice.47), channel_id=1, source_target_pairs={{0,64},{4,12},{8,72},{12,4},{16,80},{20,28},{24,88},{28,20},{32,96... | collective-permute-start | bytes 3145736 | tf_op jit(solution)/shard_map/ppermute | solution.py:65
  111.7 21.4 %collective-permute-start.15 = (f32[32,4096]{1,0:T(8,128)S(1)}, f32[32,4096]{1,0:T(8,128)S(1)}, u32[]{:S(2)}, u32[]{:S(2)}) collective-permute-start(f32[32,4096]{1,0:T(8,128)S(1)} %slice.49), channel_id=1, source_target_pairs={{0,16},{4,132},{8,24},{12,140},{16,0},{20,148},{24,8},{28,156},{32... | collective-permute-start | bytes 1572872 | tf_op jit(solution)/shard_map/ppermute | solution.py:65
  133.2 8.7 %collective-permute-start.16 = (f32[16,4096]{1,0:T(8,128)S(1)}, f32[16,4096]{1,0:T(8,128)S(1)}, u32[]{:S(2)}, u32[]{:S(2)}) collective-permute-start(f32[16,4096]{1,0:T(8,128)S(1)} %slice.51), channel_id=1, source_target_pairs={{0,128},{4,20},{8,136},{12,28},{16,144},{20,4},{24,152},{28,12},{3... | collective-permute-start | bytes 786440 | tf_op jit(solution)/shard_map/ppermute | solution.py:65
  141.9 10.4 %collective-permute-start.17 = (f32[8,4096]{1,0:T(8,128)S(1)}, f32[8,4096]{1,0:T(8,128)S(1)}, u32[]{:S(2)}, u32[]{:S(2)}) collective-permute-start(f32[8,4096]{1,0:T(8,128)S(1)} %slice.53), channel_id=1, source_target_pairs={{0,32},{4,36},{8,40},{12,44},{16,48},{20,52},{24,56},{28,60},{32,0... | collective-permute-start | bytes 393224 | tf_op jit(solution)/shard_map/ppermute | solution.py:65
  152.4 3.4 %collective-permute-start.20 = (f32[2,4096]{1,0:T(2,128)S(1)}, f32[2,4096]{1,0:T(2,128)S(1)}, u32[]{:S(2)}, u32[]{:S(2)}) collective-permute-start(f32[2,4096]{1,0:T(2,128)S(1)} %get-tuple-element.14), channel_id=1, source_target_pairs={{0,12},{4,64},{8,4},{12,72},{16,28},{20,80},{24,20},{28,88},{32,44... | collective-permute-start | bytes 98312 | tf_op jit(solution)/shard_map/ppermute | solution.py:84
  152.5 3.3 %collective-permute-start.19 = (f32[2,4096]{1,0:T(2,128)S(1)}, f32[2,4096]{1,0:T(2,128)S(1)}, u32[]{:S(2)}, u32[]{:S(2)}) collective-permute-start(f32[2,4096]{1,0:T(2,128)S(1)} %get-tuple-element.15), channel_id=1, source_target_pairs={{0,4},{4,0},{8,12},{12,8},{16,20},{20,16},{24,28},{28,24},{32,36},... | collective-permute-start | bytes 98312 | tf_op jit(solution)/shard_map/ppermute | solution.py:83
  153.8 3.9 %collective-permute-start.18 = (f32[2,4096]{1,0:T(2,128)S(1)}, f32[2,4096]{1,0:T(2,128)S(1)}, u32[]{:S(2)}, u32[]{:S(2)}) collective-permute-start(f32[2,4096]{1,0:T(2,128)S(1)} %get-tuple-element.16), channel_id=1, source_target_pairs={{0,8},{4,68},{8,0},{12,76},{16,24},{20,84},{24,16},{28,92},{32,40}... | collective-permute-start | bytes 98312 | tf_op jit(solution)/shard_map/ppermute | solution.py:82
  159.4 5.2 %collective-permute-start.21 = (f32[16,128]{1,0:T(8,128)S(1)}, f32[16,128]{1,0:T(8,128)S(1)}, u32[]{:S(2)}, u32[]{:S(2)}) collective-permute-start(f32[16,128]{1,0:T(8,128)S(1)} %fusion.24), channel_id=1, source_target_pairs={{0,1},{1,0},{2,3},{3,2},{4,5},{5,4},{6,7},{7,6},{8,9},{9,8},{10,11... | collective-permute-start | bytes 24584 | tf_op jit(solution)/shard_map/ppermute | solution.py:21
  (6 other events, 150.2 us)
